TPU v7x, 32 devices: a whole 2x2x4 slice. The times are simulated.
32 devices in a mesh: ctx: 8 (over y, x, core), tp: 4 (over z).
Axes of the slice: x: 2, y: 2, z: 4, core: 2. Of those that a mesh axis runs over, the one named last changes fastest.
Arguments:
- tokens: bfloat16 [4096, 4096], P(('ctx', 'tp')), may hold values from -6 to 6
- spike_query: int32 [4096, 32], P('ctx', 'tp'), may hold values 0 or 1
- spike_key: int32 [4096, 32], P('ctx', 'tp'), may hold values 0 or 1
- qkv_weight: bfloat16 [4096, 3, 4096], P(None, None, 'tp'), may hold values from -0.09375 to 0.09375
- qkv_blocks: int32 [3, 32, 32], P(None, None, 'tp'), may hold values 0 or 1
- out_weight: bfloat16 [4096, 4096], P('tp'), may hold values from -0.09375 to 0.09375
- out_blocks: int32 [32, 32], P('tp'), may hold values 0 or 1
- cotangent: bfloat16 [4096, 4096], P(('ctx', 'tp')), may hold values from -6 to 6
Outputs:
- layer_out: bfloat16 [4096, 4096], P(('ctx', 'tp'))
- token_grad: bfloat16 [4096, 4096], P(('ctx', 'tp'))
- qkv_grad: float32 [4096, 3, 4096], P('ctx', None, 'tp')
- out_grad: float32 [4096, 4096], P('tp', 'ctx')
All inputs are finite; a program needn't handle non-finite values. No bound on the sum of `spike_query` or of `spike_key` or of `qkv_blocks` or of `out_blocks` on one device may be relied on, other than what follows from the above.
Results may differ from a plain program's by a relative error of at most 0.014.
Values may be sent and summed in bfloat16 or wider, within the bound.
No kernel may reach another device: no remote copies, remote signals or barrier semaphores. Data moves between devices by JAX's collectives and lax.ppermute only.
A program may use at most 320 MiB of HBM per device.

v0:
```python
import math

import jax
import jax.numpy as jnp
from jax import lax
from jax.sharding import PartitionSpec as P

BLOCK = 128


EPSILON = 1e-05


def carried_in(value, axis, join, neutral):
    place = lax.axis_index(axis)
    gathered = lax.all_gather(value.astype(jnp.bfloat16), axis)
    state = jnp.zeros_like(value) + jnp.asarray(neutral, value.dtype)

    def carried_one(lap, state):
        return join(state, lax.dynamic_index_in_dim(gathered, lap, 0, False).astype(value.dtype))

    return lax.fori_loop(0, place, carried_one, state)


def entering(value, axis, join, neutral):
    count = lax.axis_size(axis)
    place = lax.axis_index(axis)
    ahead = count - 1 - place
    gathered = lax.all_gather(
        value.astype(jnp.bfloat16 if value.dtype == jnp.float32 else value.dtype), axis
    )
    state = jnp.zeros_like(value) + jnp.asarray(neutral, value.dtype)

    def entering_one(lap, state):
        source = count - 1 - lap
        return join(state, lax.dynamic_index_in_dim(gathered, source, 0, False).astype(value.dtype))

    return lax.fori_loop(0, ahead, entering_one, state)


def expand_blocks(blocks):
    row_blocks, col_blocks = blocks.shape
    spread = jnp.broadcast_to(
        blocks.astype(jnp.bfloat16)[:, None, :, None], (row_blocks, BLOCK, col_blocks, BLOCK)
    )
    return spread.reshape(row_blocks * BLOCK, col_blocks * BLOCK)


def qkv_keep_table(qkv_blocks):
    tables = [expand_blocks(qkv_blocks[projection]) for projection in range(3)]
    return jnp.stack(tables, axis=1)


def add_states(earlier, following):
    return earlier + following


def on_device(
    tokens, spike_query, spike_key, qkv_weight, qkv_blocks, out_weight, out_blocks, cotangent
):
    model_width = tokens.shape[1]
    block_rows = spike_query.shape[0]
    local_heads = spike_query.shape[1]
    features = qkv_weight.shape[2]
    head_width = features // local_heads
    highest = lax.Precision.HIGHEST
    qkv_keep = qkv_keep_table(qkv_blocks).reshape(model_width, 3 * features)
    qkv_used = qkv_weight.reshape(model_width, 3 * features) * qkv_keep
    out_used = out_weight * expand_blocks(out_blocks)
    gathered = lax.all_gather(tokens, "tp", axis=0, tiled=True)
    projected = jnp.dot(gathered, qkv_used, preferred_element_type=jnp.float32).astype(jnp.bfloat16)
    projected = projected.reshape(block_rows, 3, local_heads, head_width)
    query_spikes = spike_query.astype(jnp.bfloat16)[:, :, None]
    key_spikes = spike_key.astype(jnp.bfloat16)[:, :, None]
    query_spiked = projected[:, 0] * query_spikes
    key_spiked = projected[:, 1] * key_spikes
    values = projected[:, 2]
    query_wide = query_spiked.astype(jnp.float32)
    key_wide = key_spiked.astype(jnp.float32)
    local_state = jnp.einsum("shd,she->hde", key_spiked, values, preferred_element_type=jnp.float32)
    zeros_state = jnp.zeros_like(local_state)
    prior_state = carried_in(local_state, "ctx", add_states, zeros_state)
    positions = lax.iota(jnp.int32, block_rows)
    causal_keep = positions[:, None] >= positions[None, :]
    scores = jnp.einsum(
        "thd,shd->hts", query_spiked, key_spiked, preferred_element_type=jnp.float32
    )
    scores = jnp.where(causal_keep, scores, 0.0).astype(jnp.bfloat16)
    mixed_rows = jnp.einsum("hts,she->the", scores, values, preferred_element_type=jnp.float32)
    mixed_rows = mixed_rows + jnp.einsum("thd,hde->the", query_wide, prior_state, precision=highest)
    inv_rms = lax.rsqrt(jnp.mean(mixed_rows * mixed_rows, axis=-1, keepdims=True) + EPSILON)
    normed = mixed_rows * inv_rms
    attended = normed.astype(jnp.bfloat16).reshape(block_rows, features)
    row_piece = attended
    head_sum = lax.psum_scatter(
        jnp.dot(row_piece, out_used, preferred_element_type=jnp.float32).astype(jnp.bfloat16),
        "tp",
        scatter_dimension=0,
        tiled=True,
    ).astype(jnp.float32)
    layer_out = (tokens.astype(jnp.float32) + head_sum).astype(jnp.bfloat16)
    grad_rows = lax.all_gather(cotangent, "tp", axis=0, tiled=True)
    grad_attended = jnp.einsum("tm,fm->tf", grad_rows, out_used, preferred_element_type=jnp.float32)
    grad_attended = grad_attended.reshape(block_rows, local_heads, head_width)
    inner_mean = jnp.mean(grad_attended * normed, axis=-1, keepdims=True)
    grad_mixed = inv_rms * (grad_attended - normed * inner_mean)
    grad_low = grad_mixed.astype(jnp.bfloat16)
    local_adjoint = jnp.einsum("thd,the->hde", query_wide, grad_mixed, precision=highest)
    after_state = entering(local_adjoint, "ctx", add_states, zeros_state)
    adjoint_scores = jnp.einsum(
        "the,she->hts", grad_low, values, preferred_element_type=jnp.float32
    )
    adjoint_scores = jnp.where(causal_keep, adjoint_scores, 0.0).astype(jnp.bfloat16)
    grad_query = jnp.einsum(
        "hts,shd->thd", adjoint_scores, key_spiked, preferred_element_type=jnp.float32
    )
    grad_query = grad_query + jnp.einsum("the,hde->thd", grad_mixed, prior_state, precision=highest)
    grad_key = jnp.einsum(
        "hts,thd->shd", adjoint_scores, query_spiked, preferred_element_type=jnp.float32
    )
    grad_key = grad_key + jnp.einsum(
        "she,hde->shd", values.astype(jnp.float32), after_state, precision=highest
    )
    grad_value = jnp.einsum("hts,the->she", scores, grad_low, preferred_element_type=jnp.float32)
    grad_value = grad_value + jnp.einsum("shd,hde->she", key_wide, after_state, precision=highest)
    grad_proj = jnp.stack(
        [
            (grad_query * query_spikes.astype(jnp.float32)).astype(jnp.bfloat16),
            (grad_key * key_spikes.astype(jnp.float32)).astype(jnp.bfloat16),
            grad_value.astype(jnp.bfloat16),
        ],
        axis=1,
    ).reshape(block_rows, 3 * features)
    row_piece = grad_proj
    token_sum = lax.psum_scatter(
        jnp.einsum("tc,mc->tm", row_piece, qkv_used, preferred_element_type=jnp.float32).astype(
            jnp.bfloat16
        ),
        "tp",
        scatter_dimension=0,
        tiled=True,
    ).astype(jnp.float32)
    token_grad = (cotangent.astype(jnp.float32) + token_sum).astype(jnp.bfloat16)
    out_keep_cols = expand_blocks(jnp.transpose(out_blocks))
    slice_rows = model_width // lax.axis_size("ctx")
    norm_factor = 1.0 / math.sqrt(block_rows * lax.axis_size("ctx"))
    qkv_part = jnp.einsum("tm,tc->mc", gathered, grad_proj, preferred_element_type=jnp.float32)
    qkv_part = qkv_part * qkv_keep
    out_part = jnp.einsum("tm,tf->mf", grad_rows, attended, preferred_element_type=jnp.float32)
    out_part = out_part * out_keep_cols
    weight_sum = lax.psum_scatter(
        jnp.concatenate([qkv_part, out_part], axis=1).astype(jnp.bfloat16),
        "ctx",
        scatter_dimension=0,
        tiled=True,
    ).astype(jnp.float32)
    weight_sum = weight_sum * norm_factor
    qkv_grad = weight_sum[:, : 3 * features].reshape(slice_rows, 3, features)
    out_grad = jnp.transpose(weight_sum[:, 3 * features :])
    return (layer_out, token_grad, qkv_grad, out_grad)


def solution(mesh):
    placed = (
        P(("ctx", "tp"), None),
        P("ctx", "tp"),
        P("ctx", "tp"),
        P(None, None, "tp"),
        P(None, None, "tp"),
        P("tp", None),
        P("tp", None),
        P(("ctx", "tp"), None),
    )
    return jax.shard_map(
        on_device,
        mesh=mesh,
        in_specs=placed,
        out_specs=(
            P(("ctx", "tp"), None),
            P(("ctx", "tp"), None),
            P("ctx", None, "tp"),
            P("tp", "ctx"),
        ),
        check_vma=False,
    )
```

profile of v0, /device:TPU:0, one launch (start us, length us, event | category | flops | bytes accessed | tf_op | source)
XLA Modules:
  0.0 714.8 jit_solution(4649358727200529671)
XLA Ops:
  8.0 32.2 %copy.43 = bf16[4096,3,1024]{0,2,1:T(8,128)(2,1)} copy(bf16[4096,3,1024]{2,0,1:T(8,128)(2,1)} %param.15) | data formatting | bytes 50331648 | tf_op args[3]
  40.2 4.5 broadcast_in_dim.22
  44.7 13.3 %stack_reshape.9 = bf16[4096,1,1024]{0,2,1:T(8,128)(2,1)} reshape(bf16[32,128,8,128]{1,0,3,2:T(8,128)(2,1)} %broadcast_in_dim.22) | data formatting | bytes 16777216 | tf_op jit(solution)/shard_map/stack;reshape | solution.py:51
  58.0 4.5 broadcast_in_dim.25
  62.5 13.3 %stack_reshape.10 = bf16[4096,1,1024]{0,2,1:T(8,128)(2,1)} reshape(bf16[32,128,8,128]{1,0,3,2:T(8,128)(2,1)} %broadcast_in_dim.25) | data formatting | bytes 16777216 | tf_op jit(solution)/shard_map/stack;reshape | solution.py:51
  80.3 13.4 %stack_reshape.11 = bf16[4096,1,1024]{0,2,1:T(8,128)(2,1)} reshape(bf16[32,128,8,128]{1,0,3,2:T(8,128)(2,1)} %broadcast_in_dim.26) | data formatting | bytes 16777216 | tf_op jit(solution)/shard_map/stack;reshape | solution.py:51
  93.7 7.8 %constant_dynamic-update-slice_fusion.2 = bf16[4096,3,1024]{0,2,1:T(8,128)(2,1)} fusion(bf16[4096,1,1024]{0,2,1:T(8,128)(2,1)} %stack_reshape.9), kind=kLoop, calls=%fused_computation.51 | loop fusion | bytes 16777216
  101.5 7.7 %constant_dynamic-update-slice_fusion.1 = bf16[4096,3,1024]{0,2,1:T(8,128)(2,1)} fusion(bf16[4096,3,1024]{0,2,1:T(8,128)(2,1)} %constant_dynamic-update-slice_fusion.2, bf16[4096,1,1024]{0,2,1:T(8,128)(2,1)} %stack_reshape.10), kind=kLoop, calls=%fused_computation.50 | loop fusion | bytes 16777216
  109.2 7.8 %constant_dynamic-update-slice_fusion = bf16[4096,3,1024]{0,2,1:T(8,128)(2,1)} fusion(bf16[4096,3,1024]{0,2,1:T(8,128)(2,1)} %constant_dynamic-update-slice_fusion.1, bf16[4096,1,1024]{0,2,1:T(8,128)(2,1)} %stack_reshape.11), kind=kLoop, calls=%fused_computation.49 | loop fusion | bytes 16777216 | tf_op jit(solution)/shard_map/stack | solution.py:51
  117.0 28.6 %mul.82 = bf16[4096,3,1024]{0,2,1:T(8,128)(2,1)} multiply(bf16[4096,3,1024]{0,2,1:T(8,128)(2,1)} %copy.43, bf16[4096,3,1024]{0,2,1:T(8,128)(2,1)} %constant_dynamic-update-slice_fusion) | non-fusion elementwise | flops 12582912 | bytes 75497472 | tf_op jit(solution)/shard_map/mul | solution.py:68
  145.7 18.2 %convolution_convert_fusion.2 = bf16[3072,512]{1,0:T(8,128)(2,1)S(1)} fusion(bf16[4096,3072]{0,1:T(8,128)(2,1)} %bitcast.148, bf16[512,4096]{1,0:T(8,128)(2,1)} %all-gather.7.cloned.1.call-done), kind=kOutput, calls=%fused_computation.13 | convolution fusion | flops 12886474752 | bytes 32505856 | tf_op jit(solution)/shard_map/dot_general | solution.py:71
  173.0 22.5 %all-gather.11.cloned.1.call-done = bf16[64,128,128]{2,1,0:T(8,128)(2,1)} async-done(((bf16[8,128,128]{2,1,0:T(8,128)(2,1)}), bf16[64,128,128]{2,1,0:T(8,128)(2,1)}) %all-gather.11.cloned.1.call-update) | async-done | bytes 2097168 | tf_op jit(solution)/shard_map/all_gather | solution.py:16
  198.6 79.2 %all-gather.9.cloned.1.call-done = bf16[512,4096]{1,0:T(8,128)(2,1)} async-done(((bf16[128,4096]{1,0:T(8,128)(2,1)}), bf16[512,4096]{1,0:T(8,128)(2,1)}) %all-gather.9.cloned.1.call-update) | async-done | bytes 4194320 | tf_op jit(solution)/shard_map/all_gather | solution.py:102
  279.0 12.4 %multiply_reduce_fusion = (f32[512,8]{0,1:T(8,128)S(1)}, f32[1024,512]{1,0:T(8,128)S(1)}) fusion(f32[8,128,512]{2,1,0:T(8,128)S(1)} %get-tuple-element.125, f32[512,8]{0,1:T(8,128)S(1)} %add_rsqrt_fusion, bf16[512,4096]{1,0:T(8,128)(2,1)} %all-gather.9.cloned.1.call-done, bf16[1024,4096]{1,0:T(8,128)(2,1)} %param.17, bf16[128,8,32,128]{3,2,1,0:T(8,128)(2,1)S(1)} %bitcast.145), kind=kOutput, calls=%fused_computation.27 | convolution fusion | flops 4300730368 | bytes 25198592 | tf_op jit(solution)/shard_map/tm,fm->tf/dot_general | solution.py:103
  297.9 13.5 %convolution_convert_fusion.1 = bf16[512,4096]{1,0:T(8,128)(2,1)} fusion(bf16[512,1024]{0,1:T(8,128)(2,1)} %bitcast.160, bf16[1024,4096]{1,0:T(8,128)(2,1)} %param.17, bf16[128,8,32,128]{3,2,1,0:T(8,128)(2,1)} %bitcast.146), kind=kOutput, calls=%fused_computation.12 | convolution fusion | flops 4301258752 | bytes 22020096 | tf_op jit(solution)/shard_map/dot_general | solution.py:96
  324.3 8.0 %while.23 = (s32[]{:T(128)}, f32[8,128,128]{2,1,0:T(8,128)S(1)}, s32[]{:T(128)}, bf16[8,8,128,128]{3,2,1,0:T(8,128)(2,1)}, s32[]{:T(128)}, /*index=5*/s32[]{:T(128)}, s32[]{:T(128)}, s32[]{:T(128)}) while((s32[]{:T(128)}, f32[8,128,128]{2,1,0:T(8,128)S(1)}, s32[]{:T(128)}, bf16[8,8,128,128]{3,2,1,0:T(8,128)(2,1)}, s32[]{:T(128)}, ...), condition=%wide.region_6.7_spmd, body=%wide.region_5.6_spmd.sunk | while | flops 262150 | bytes 1310863 | solution.py:38
  340.3 19.9 %convolution_convert_fusion = bf16[512,4096]{1,0:T(8,128)(2,1)} fusion(bf16[512,3072]{0,1:T(8,128)(2,1)S(1)} %bitcast.162, bf16[4096,3072]{0,1:T(8,128)(2,1)} %bitcast.149), kind=kOutput, calls=%fused_computation.11 | convolution fusion | flops 12886999040 | bytes 32505856 | tf_op jit(solution)/shard_map/tc,mc->tm/dot_general | solution.py:136
  360.2 8.0 %broadcast_in_dim.58 = f32[32,128,8,128]{1,0,3,2:T(8,128)} broadcast(f32[32,8]{0,1:T(8,128)S(1)} %get-tuple-element.113), dimensions={0,2} | broadcast | bytes 16778240 | tf_op jit(solution)/shard_map/broadcast_in_dim | solution.py:43
  368.2 15.6 %fusion.1 = bf16[4096,1024]{0,1:T(8,128)(2,1)} fusion(f32[128,8,32,128]{3,2,1,0:T(8,128)} %bitcast.143, bf16[512,1024]{0,1:T(8,128)(2,1)S(1)} %bitcast.161, bf16[512,4096]{1,0:T(8,128)(2,1)S(1)} %copy-done.6), kind=kOutput, calls=%fused_computation.6 | convolution fusion | flops 4303355904 | bytes 30408704 | tf_op jit(solution)/shard_map/tm,tf->mf/dot_general | solution.py:149
  383.8 27.2 %fusion = bf16[4096,3072]{0,1:T(8,128)(2,1)} fusion(bf16[4096,3072]{0,1:T(8,128)(2,1)} %bitcast.144, bf16[512,3072]{0,1:T(8,128)(2,1)} %bitcast.163, bf16[512,4096]{1,0:T(8,128)(2,1)} %all-gather.7.cloned.1.call-done), kind=kOutput, calls=%fused_computation.3 | convolution fusion | flops 12922650624 | bytes 57671680 | tf_op jit(solution)/shard_map/tm,tc->mc/dot_general | solution.py:147
  411.0 24.2 %pad_maximum_fusion = bf16[4096,4096]{0,1:T(8,128)(2,1)} fusion(bf16[4096,1024]{0,1:T(8,128)(2,1)} %fusion.1, bf16[4096,3072]{0,1:T(8,128)(2,1)} %fusion), kind=kLoop, calls=%fused_computation.4 | loop fusion | flops 67108864 | bytes 67108864 | tf_op jit(solution)/shard_map/concatenate | solution.py:152
  438.8 44.5 %reduce-scatter.6.cloned.1.call-done = bf16[128,4096]{1,0:T(8,128)(2,1)} async-done(((bf16[512,4096]{1,0:T(8,128)(2,1)}), bf16[128,4096]{1,0:T(8,128)(2,1)}) %reduce-scatter.6.cloned.1.call-update) | async-done | bytes 1048592 | tf_op jit(solution)/shard_map/reduce_scatter | solution.py:135
  485.8 206.9 %reduce-scatter.8.cloned.1.call-done = bf16[512,4096]{0,1:T(8,128)(2,1)} async-done(((bf16[4096,4096]{0,1:T(8,128)(2,1)}), bf16[512,4096]{0,1:T(8,128)(2,1)}) %reduce-scatter.8.cloned.1.call-update) | async-done | bytes 4194320 | tf_op jit(solution)/shard_map/reduce_scatter | solution.py:151
  700.9 6.6 copy.56
  (89 shorter events, 67.8 us)
Async XLA Ops:
  7.2 138.5 %all-gather.7.cloned.1.call-start = ((), (), s32[]{:S(2)}) async-start(), calls=%async_computation.3 | async-start | bytes 5242880 | tf_op jit(solution)/shard_map/all_gather | solution.py:70
  7.9 32.3 %copy-start.15 = (s32[3,32,8]{1,2,0:T(8,128)S(1)}, s32[3,32,8]{1,2,0:T(8,128)}, u32[]{:S(2)}) copy-start(s32[3,32,8]{1,2,0:T(8,128)} %param.16) | copy-start | bytes 9220
  7.9 187.5 %all-gather.11.cloned.1.call-start = ((), (), s32[]{:S(2)}) async-start(), calls=%async_computation.8 | async-start | bytes 2359296 | tf_op jit(solution)/shard_map/all_gather | solution.py:16
  117.0 28.6 %copy-start.13 = (s32[512,8]{0,1:T(8,128)S(1)}, s32[512,8]{0,1:T(8,128)}, u32[]{:S(2)}) copy-start(s32[512,8]{0,1:T(8,128)} %param.13) | copy-start | bytes 49156
  117.0 28.6 %copy-start.14 = (s32[512,8]{0,1:T(8,128)S(1)}, s32[512,8]{0,1:T(8,128)}, u32[]{:S(2)}) copy-start(s32[512,8]{0,1:T(8,128)} %param.14) | copy-start | bytes 49156
  163.8 4.3 copy-start.1
  163.9 2.9 copy-start.16
  165.4 112.4 %all-gather.9.cloned.1.call-start = ((), (), s32[]{:S(2)}) async-start(), calls=%async_computation.5 | async-start | bytes 5242880 | tf_op jit(solution)/shard_map/all_gather | solution.py:102
  166.1 158.2 %all-gather.13.cloned.1.call-start = ((), (), s32[]{:S(2)}) async-start(), calls=%async_computation.9 | async-start | bytes 2359296 | tf_op jit(solution)/shard_map/all_gather | solution.py:29
  168.2 2.0 copy-start.4
  198.6 80.4 %copy-start.3 = (f32[8,128,512]{2,1,0:T(8,128)}, f32[8,128,512]{2,1,0:T(8,128)S(1)}, u32[]{:S(2)}) copy-start(f32[8,128,512]{2,1,0:T(8,128)S(1)} %get-tuple-element.125) | copy-start | bytes 6291460
  279.0 12.4 %copy-start = (bf16[8,128,32,128]{3,2,1,0:T(8,128)(2,1)}, bf16[8,128,32,128]{3,2,1,0:T(8,128)(2,1)S(1)}, u32[]{:S(2)}) copy-start(bf16[8,128,32,128]{3,2,1,0:T(8,128)(2,1)S(1)} %broadcast_in_dim.30) | copy-start | bytes 25165828
  297.7 137.5 %reduce-scatter.4.cloned.1.call-start = ((), (), s32[]{:S(2)}) async-start(), calls=%async_computation.4 | async-start | bytes 5242880 | tf_op jit(solution)/shard_map/reduce_scatter | solution.py:95
  311.4 171.9 %reduce-scatter.6.cloned.1.call-start = ((), (), s32[]{:S(2)}) async-start(), calls=%async_computation.6 | async-start | bytes 5242880 | tf_op jit(solution)/shard_map/reduce_scatter | solution.py:135
  311.5 2.7 copy-start.2
  318.6 3.0 copy-start.5
  324.3 11.7 %copy-start.7 = (f32[8,128,512]{2,1,0:T(8,128)S(1)}, f32[8,128,512]{2,1,0:T(8,128)}, u32[]{:S(2)}) copy-start(f32[8,128,512]{2,1,0:T(8,128)} %fusion.17) | copy-start | bytes 6291460
  332.4 5.9 copy-start.11
  338.6 1.6 copy-start.12
  360.2 332.5 %reduce-scatter.8.cloned.1.call-start = ((), (), s32[]{:S(2)}) async-start(), calls=%async_computation.7 | async-start | bytes 37748736 | tf_op jit(solution)/shard_map/reduce_scatter | solution.py:151
  360.2 8.0 %copy-start.6 = (bf16[512,4096]{1,0:T(8,128)(2,1)S(1)}, bf16[512,4096]{1,0:T(8,128)(2,1)}, u32[]{:S(2)}) copy-start(bf16[512,4096]{1,0:T(8,128)(2,1)} %all-gather.9.cloned.1.call-done) | copy-start | bytes 12582916
  360.2 8.0 %copy-start.8 = (bf16[512,8,128]{0,2,1:T(8,128)(2,1)S(1)}, bf16[512,8,128]{0,2,1:T(8,128)(2,1)}, u32[]{:S(2)}) copy-start(bf16[512,8,128]{0,2,1:T(8,128)(2,1)} %get-tuple-element.120) | copy-start | bytes 3145732
  435.2 1.2 copy-start.9
  435.2 48.2 %copy-start.10 = (bf16[128,4096]{1,0:T(8,128)(2,1)S(1)}, bf16[128,4096]{1,0:T(8,128)(2,1)}, u32[]{:S(2)}) copy-start(bf16[128,4096]{1,0:T(8,128)(2,1)} %param.19) | copy-start | bytes 3145732
Sparse Core Ops, SparseCore 0:
  9.6 83.4 all-gather.6
  165.5 29.8 all-gather.10
  197.0 80.7 all-gather.8
  297.8 26.4 all-gather.12
  327.0 76.7 reduce-scatter.3
  406.1 77.2 reduce-scatter.5
  486.9 205.7 reduce-scatter.7
where the time goes:
time: 725 us; the launch traced here: 715 us
  waiting for transfers between devices  355 us (49%)
  matrix products  136 us (19%)
  local copies, waits for them, and re-layouts  135 us (19%)
  other arithmetic  72.3 us (10%)
  between operations  14.9 us (2%)
    reduce_scatter x1, waiting for transfers between devices, on_device(): lax.psum_scatter(jnp.concatenate([qkv_part, out_part], axis=1).astype(jnp...  207 us
    all_gather x1, waiting for transfers between devices, on_device(): grad_rows = lax.all_gather(cotangent, 'tp', axis=0, tiled=True)  79.2 us
    unnamed x38, local copies, waits for them, and re-layouts  60 us
    another operation x4, local copies, waits for them, and re-layouts, qkv_keep_table(): return jnp.stack(tables, axis=1)  47.8 us
    reduce_scatter x1, waiting for transfers between devices, on_device(): lax.psum_scatter(jnp.einsum('tc,mc->tm', row_piece, qkv_used, preferred_e...  44.5 us
    mul x1, other arithmetic, on_device(): qkv_used = qkv_weight.reshape(model_width, 3 * features) * qkv_keep  28.6 us
    dot_general x1, matrix products, on_device(): jnp.einsum('tm,tc->mc', gathered, grad_proj, preferred_element_type=jnp.f...  27.2 us
    concatenate x1, other arithmetic, on_device(): jnp.concatenate([qkv_part, out_part], axis=1).astype(jnp.bfloat16)  24.2 us
  transfers between devices with their start and end apart: 7, of which 5 were waited for; matrix products, arithmetic and copies ran while one was open for 40% of the time, Pallas kernels for 0%

commit v1 on v0

--- a/solution.py
+++ b/solution.py
@@ -63,10 +63,18 @@
     local_heads = spike_query.shape[1]
     features = qkv_weight.shape[2]
     head_width = features // local_heads
+    row_blocks = model_width // BLOCK
+    col_blocks = features // BLOCK
     highest = lax.Precision.HIGHEST
-    qkv_keep = qkv_keep_table(qkv_blocks).reshape(model_width, 3 * features)
-    qkv_used = qkv_weight.reshape(model_width, 3 * features) * qkv_keep
-    out_used = out_weight * expand_blocks(out_blocks)
+    qkv_mask = jnp.transpose(qkv_blocks, (1, 0, 2)).astype(jnp.bfloat16)
+    qkv_used = (
+        qkv_weight.reshape(row_blocks, BLOCK, 3, col_blocks, BLOCK)
+        * qkv_mask[:, None, :, :, None]
+    ).reshape(model_width, 3 * features)
+    out_used = (
+        out_weight.reshape(col_blocks, BLOCK, row_blocks, BLOCK)
+        * out_blocks.astype(jnp.bfloat16)[:, None, :, None]
+    ).reshape(features, model_width)
     gathered = lax.all_gather(tokens, "tp", axis=0, tiled=True)
     projected = jnp.dot(gathered, qkv_used, preferred_element_type=jnp.float32).astype(jnp.bfloat16)
     projected = projected.reshape(block_rows, 3, local_heads, head_width)
@@ -91,15 +99,29 @@
     inv_rms = lax.rsqrt(jnp.mean(mixed_rows * mixed_rows, axis=-1, keepdims=True) + EPSILON)
     normed = mixed_rows * inv_rms
     attended = normed.astype(jnp.bfloat16).reshape(block_rows, features)
-    row_piece = attended
     head_sum = lax.psum_scatter(
-        jnp.dot(row_piece, out_used, preferred_element_type=jnp.float32).astype(jnp.bfloat16),
+        jnp.dot(attended, out_used, preferred_element_type=jnp.float32).astype(jnp.bfloat16),
         "tp",
         scatter_dimension=0,
         tiled=True,
     ).astype(jnp.float32)
     layer_out = (tokens.astype(jnp.float32) + head_sum).astype(jnp.bfloat16)
     grad_rows = lax.all_gather(cotangent, "tp", axis=0, tiled=True)
+    ctx_count = lax.axis_size("ctx")
+    ctx_place = lax.axis_index("ctx")
+    slice_rows = model_width // ctx_count
+    slice_blocks = slice_rows // BLOCK
+    norm_factor = 1.0 / math.sqrt(block_rows * ctx_count)
+    out_part = jnp.einsum("tm,tf->mf", grad_rows, attended, preferred_element_type=jnp.float32)
+    out_sum = lax.psum_scatter(
+        out_part.astype(jnp.bfloat16), "ctx", scatter_dimension=0, tiled=True
+    ).astype(jnp.float32)
+    out_keep = lax.dynamic_slice_in_dim(out_blocks, ctx_place * slice_blocks, slice_blocks, 1)
+    out_keep = jnp.broadcast_to(
+        jnp.transpose(out_keep).astype(jnp.float32)[:, None, :, None],
+        (slice_blocks, BLOCK, col_blocks, BLOCK),
+    ).reshape(slice_rows, features)
+    out_grad = jnp.transpose(out_sum * out_keep * norm_factor)
     grad_attended = jnp.einsum("tm,fm->tf", grad_rows, out_used, preferred_element_type=jnp.float32)
     grad_attended = grad_attended.reshape(block_rows, local_heads, head_width)
     inner_mean = jnp.mean(grad_attended * normed, axis=-1, keepdims=True)
@@ -131,9 +153,18 @@
         ],
         axis=1,
     ).reshape(block_rows, 3 * features)
-    row_piece = grad_proj
+    qkv_part = jnp.einsum("tm,tc->mc", gathered, grad_proj, preferred_element_type=jnp.float32)
+    qkv_sum = lax.psum_scatter(
+        qkv_part.astype(jnp.bfloat16), "ctx", scatter_dimension=0, tiled=True
+    ).astype(jnp.float32)
+    qkv_keep = lax.dynamic_slice_in_dim(qkv_mask, ctx_place * slice_blocks, slice_blocks, 0)
+    qkv_keep = jnp.broadcast_to(
+        qkv_keep.astype(jnp.float32)[:, None, :, :, None],
+        (slice_blocks, BLOCK, 3, col_blocks, BLOCK),
+    ).reshape(slice_rows, 3, features)
+    qkv_grad = qkv_sum.reshape(slice_rows, 3, features) * qkv_keep * norm_factor
     token_sum = lax.psum_scatter(
-        jnp.einsum("tc,mc->tm", row_piece, qkv_used, preferred_element_type=jnp.float32).astype(
+        jnp.einsum("tc,mc->tm", grad_proj, qkv_used, preferred_element_type=jnp.float32).astype(
             jnp.bfloat16
         ),
         "tp",
@@ -141,22 +172,6 @@
         tiled=True,
     ).astype(jnp.float32)
     token_grad = (cotangent.astype(jnp.float32) + token_sum).astype(jnp.bfloat16)
-    out_keep_cols = expand_blocks(jnp.transpose(out_blocks))
-    slice_rows = model_width // lax.axis_size("ctx")
-    norm_factor = 1.0 / math.sqrt(block_rows * lax.axis_size("ctx"))
-    qkv_part = jnp.einsum("tm,tc->mc", gathered, grad_proj, preferred_element_type=jnp.float32)
-    qkv_part = qkv_part * qkv_keep
-    out_part = jnp.einsum("tm,tf->mf", grad_rows, attended, preferred_element_type=jnp.float32)
-    out_part = out_part * out_keep_cols
-    weight_sum = lax.psum_scatter(
-        jnp.concatenate([qkv_part, out_part], axis=1).astype(jnp.bfloat16),
-        "ctx",
-        scatter_dimension=0,
-        tiled=True,
-    ).astype(jnp.float32)
-    weight_sum = weight_sum * norm_factor
-    qkv_grad = weight_sum[:, : 3 * features].reshape(slice_rows, 3, features)
-    out_grad = jnp.transpose(weight_sum[:, 3 * features :])
     return (layer_out, token_grad, qkv_grad, out_grad)
 
 

time: 725 us -> 775 us (1.069)
  local copies, waits for them, and re-layouts: 135 us -> 179 us
  matrix products: 136 us -> 122 us
  other arithmetic: 72.3 us -> 83.5 us
  waiting for transfers between devices: 355 us -> 365 us
    mul x0 -> x6, local copies, waits for them, and re-layouts: none -> 125 us  [the longest x5 124 us: on_device(): qkv_weight.reshape(row_blocks, BLOCK, 3, col_blocks, BLOCK)]
    another operation x4 -> x0, local copies, waits for them, and re-layouts: 47.8 us -> none  [qkv_keep_table(): return jnp.stack(tables, axis=1)]
    mul x2 -> x3, other arithmetic: 31.9 us -> 63.7 us  [the longest x2 54.1 us: on_device(): qkv_weight.reshape(row_blocks, BLOCK, 3, col_blocks, BLOCK)]
    concatenate x1 -> x0, other arithmetic: 24.2 us -> none  [on_device(): jnp.concatenate([qkv_part, out_part], axis=1).astype(jnp.bfloat16)]
    unnamed x38 -> x31, local copies, waits for them, and re-layouts: 60 us -> 37.1 us
    broadcast_in_dim x5 -> x2, local copies, waits for them, and re-layouts: 22.6 us -> 3.51 us  [the longest x1 3.18 us: on_device(): jnp.broadcast_to(qkv_keep.astype(jnp.float32)[:, None, :, :, None], (slic...]
    reshape x0 -> x2, local copies, waits for them, and re-layouts: none -> 12.5 us  [the longest x1 7.15 us: on_device(): qkv_keep = jnp.broadcast_to(qkv_keep.astype(jnp.float32)[:, None, :, :, N...]
    reduce_scatter x3 -> x4, waiting for transfers between devices: 251 us -> 260 us  [the longest x1 158 us: on_device(): lax.psum_scatter(qkv_part.astype(jnp.bfloat16), 'ctx', scatter_dimension=...]
  transfers between devices with their start and end apart: 7 -> 8, of which waited for: 5 -> 5; matrix products, arithmetic and copies ran while one was open for 40% -> 43% of each run, Pallas kernels for 0% -> 0%
where the time goes in v1:
time: 775 us; the launch traced here: 765 us
  waiting for transfers between devices  365 us (47%)
  local copies, waits for them, and re-layouts  179 us (23%)
  matrix products  122 us (16%)
  other arithmetic  83.5 us (11%)
  between operations  14.6 us (2%)
    reduce_scatter x1, waiting for transfers between devices, on_device(): lax.psum_scatter(qkv_part.astype(jnp.bfloat16), 'ctx', scatter_dimension=...  158 us
    mul x5, local copies, waits for them, and re-layouts, on_device(): qkv_weight.reshape(row_blocks, BLOCK, 3, col_blocks, BLOCK)  124 us
    all_gather x1, waiting for transfers between devices, on_device(): grad_rows = lax.all_gather(cotangent, 'tp', axis=0, tiled=True)  79 us
    reduce_scatter x1, waiting for transfers between devices, on_device(): lax.psum_scatter(out_part.astype(jnp.bfloat16), 'ctx', scatter_dimension=...  72.9 us
    mul x2, other arithmetic, on_device(): qkv_weight.reshape(row_blocks, BLOCK, 3, col_blocks, BLOCK)  54.1 us
    unnamed x31, local copies, waits for them, and re-layouts  37.1 us
    reduce_scatter x1, waiting for transfers between devices, on_device(): lax.psum_scatter(jnp.einsum('tc,mc->tm', grad_proj, qkv_used, preferred_e...  29.9 us
    all_gather x1, waiting for transfers between devices, carried_in(): gathered = lax.all_gather(value.astype(jnp.bfloat16), axis)  23.8 us
  transfers between devices with their start and end apart: 8, of which 5 were waited for; matrix products, arithmetic and copies ran while one was open for 43% of the time, Pallas kernels for 0%

profile of v1, /device:TPU:0, one launch (start us, length us, event | category | flops | bytes accessed | tf_op | source)
XLA Modules:
  0.0 764.6 jit_solution(3684629579513583311)
XLA Ops:
  8.8 8.7 %mul.111 = bf16[32,128,3,8,128]{4,3,2,1,0:T(8,128)(2,1)} broadcast(bf16[32,3,8]{2,1,0:T(4,128)(2,1)S(1)} %copy.47), dimensions={0,2,3} | broadcast | bytes 25167360 | tf_op jit(solution)/shard_map/mul | solution.py:71
  17.5 37.4 %mul.112 = bf16[4096,3072]{1,0:T(8,128)(2,1)} reshape(bf16[32,128,3,8,128]{4,3,2,1,0:T(8,128)(2,1)} %mul.111) | data formatting | bytes 50331648 | tf_op jit(solution)/shard_map/mul | solution.py:71
  54.9 31.5 %copy.48 = bf16[4096,3072]{0,1:T(8,128)(2,1)} copy(bf16[4096,3072]{1,0:T(8,128)(2,1)} %mul.112) | data formatting | bytes 50331648 | tf_op jit(solution)/shard_map/mul | solution.py:71
  86.4 33.6 %copy.46 = bf16[4096,3,1024]{0,2,1:T(8,128)(2,1)} copy(bf16[4096,3,1024]{2,0,1:T(8,128)(2,1)} %param.15) | data formatting | bytes 50331648 | tf_op args[3]
  120.0 25.4 %bitcast_multiply_fusion = bf16[4096,3072]{0,1:T(8,128)(2,1)} fusion(bf16[4096,3072]{0,1:T(8,128)(2,1)} %copy.48, bf16[4096,3,1024]{0,2,1:T(8,128)(2,1)} %copy.46), kind=kLoop, calls=%fused_computation.2 | loop fusion | flops 12582912 | bytes 75497472 | tf_op jit(solution)/shard_map/mul | solution.py:71
  145.4 18.2 %convolution_convert_fusion.2 = bf16[3072,512]{1,0:T(8,128)(2,1)S(1)} fusion(bf16[4096,3072]{0,1:T(8,128)(2,1)} %bitcast_multiply_fusion, bf16[512,4096]{1,0:T(8,128)(2,1)} %all-gather.7.cloned.1.call-done), kind=kOutput, calls=%fused_computation.11 | convolution fusion | flops 12886474752 | bytes 32505856 | tf_op jit(solution)/shard_map/dot_general | solution.py:79
  172.3 23.8 %all-gather.11.cloned.1.call-done = bf16[64,128,128]{2,1,0:T(8,128)(2,1)} async-done(((bf16[8,128,128]{2,1,0:T(8,128)(2,1)}), bf16[64,128,128]{2,1,0:T(8,128)(2,1)}) %all-gather.11.cloned.1.call-update) | async-done | bytes 2097168 | tf_op jit(solution)/shard_map/all_gather | solution.py:16
  199.5 79.0 %all-gather.9.cloned.1.call-done = bf16[512,4096]{1,0:T(8,128)(2,1)} async-done(((bf16[128,4096]{1,0:T(8,128)(2,1)}), bf16[512,4096]{1,0:T(8,128)(2,1)}) %all-gather.9.cloned.1.call-update) | async-done | bytes 4194320 | tf_op jit(solution)/shard_map/all_gather | solution.py:109
  279.6 12.4 %multiply_reduce_fusion = (f32[512,8]{0,1:T(8,128)S(1)}, f32[1024,512]{1,0:T(8,128)S(1)}) fusion(f32[8,128,512]{2,1,0:T(8,128)S(1)} %get-tuple-element.108, f32[512,8]{0,1:T(8,128)S(1)} %add_rsqrt_fusion, bf16[512,4096]{1,0:T(8,128)(2,1)} %all-gather.9.cloned.1.call-done, bf16[1024,4096]{1,0:T(8,128)(2,1)} %param.17, bf16[128,8,32,128]{3,2,1,0:T(8,128)(2,1)S(1)} %bitcast.142), kind=kOutput, calls=%fused_computation.27 | convolution fusion | flops 4300730368 | bytes 25198592 | tf_op jit(solution)/shard_map/tm,fm->tf/dot_general | solution.py:125
  298.8 13.4 %convolution_convert_fusion.1 = bf16[512,4096]{1,0:T(8,128)(2,1)} fusion(bf16[512,1024]{0,1:T(8,128)(2,1)} %bitcast.159, bf16[1024,4096]{1,0:T(8,128)(2,1)} %param.17, bf16[128,8,32,128]{3,2,1,0:T(8,128)(2,1)} %bitcast.143), kind=kOutput, calls=%fused_computation.10 | convolution fusion | flops 4301258752 | bytes 22020096 | tf_op jit(solution)/shard_map/dot_general | solution.py:103
  312.3 8.8 %mul.111.clone = bf16[32,128,3,8,128]{1,0,4,3,2:T(8,128)(2,1)} broadcast(bf16[32,3,8]{0,2,1:T(8,128)(2,1)S(1)} %convert_bitcast_fusion.4), dimensions={0,2,3} | broadcast | bytes 25167360 | tf_op jit(solution)/shard_map/mul | solution.py:71
  321.1 37.5 %mul.132 = bf16[4096,3,1024]{0,2,1:T(8,128)(2,1)} reshape(bf16[32,128,3,8,128]{1,0,4,3,2:T(8,128)(2,1)} %mul.111.clone) | data formatting | bytes 50331648 | tf_op jit(solution)/shard_map/mul | solution.py:71
  358.7 28.7 %mul.133 = bf16[4096,3,1024]{0,2,1:T(8,128)(2,1)} multiply(bf16[4096,3,1024]{0,2,1:T(8,128)(2,1)} %copy.46, bf16[4096,3,1024]{0,2,1:T(8,128)(2,1)} %mul.132) | non-fusion elementwise | flops 12582912 | bytes 75497472 | tf_op jit(solution)/shard_map/mul | solution.py:71
  399.5 7.8 %while.23 = (s32[]{:T(128)}, f32[8,128,128]{2,1,0:T(8,128)S(1)}, s32[]{:T(128)}, bf16[8,8,128,128]{3,2,1,0:T(8,128)(2,1)}, s32[]{:T(128)}, /*index=5*/s32[]{:T(128)}, s32[]{:T(128)}, s32[]{:T(128)}) while((s32[]{:T(128)}, f32[8,128,128]{2,1,0:T(8,128)S(1)}, s32[]{:T(128)}, bf16[8,8,128,128]{3,2,1,0:T(8,128)(2,1)}, s32[]{:T(128)}, ...), condition=%wide.region_6.7_spmd, body=%wide.region_5.6_spmd.sunk | while | flops 262150 | bytes 1310863 | solution.py:38
  413.3 19.5 %convolution_convert_fusion = bf16[512,4096]{1,0:T(8,128)(2,1)} fusion(bf16[512,3072]{0,1:T(8,128)(2,1)S(1)} %bitcast.156, bf16[4096,3072]{0,1:T(8,128)(2,1)} %bitcast.144), kind=kOutput, calls=%fused_computation.9 | convolution fusion | flops 12886999040 | bytes 32505856 | tf_op jit(solution)/shard_map/tc,mc->tm/dot_general | solution.py:167
  433.1 10.4 %convert_bitcast_fusion.1 = bf16[4096,1024]{0,1:T(8,128)(2,1)} fusion(bf16[512,1024]{0,1:T(8,128)(2,1)} %bitcast.160, bf16[512,4096]{1,0:T(8,128)(2,1)} %all-gather.9.cloned.1.call-done), kind=kOutput, calls=%fused_computation.5 | convolution fusion | flops 4299161600 | bytes 13631488 | tf_op jit(solution)/shard_map/tm,tf->mf/dot_general | solution.py:115
  443.5 19.1 %convert_bitcast_fusion = bf16[4096,3072]{0,1:T(8,128)(2,1)} fusion(bf16[512,3072]{0,1:T(8,128)(2,1)S(1)} %bitcast.157, bf16[512,4096]{1,0:T(8,128)(2,1)} %all-gather.7.cloned.1.call-done), kind=kOutput, calls=%fused_computation.3 | convolution fusion | flops 12897484800 | bytes 32505856 | tf_op jit(solution)/shard_map/tm,tc->mc/dot_general | solution.py:156
  463.5 3.2 broadcast_in_dim.38
  466.7 7.2 reshape.76
  476.5 29.9 %reduce-scatter.7.cloned.1.call-done = bf16[128,4096]{1,0:T(8,128)(2,1)} async-done(((bf16[512,4096]{1,0:T(8,128)(2,1)}), bf16[128,4096]{1,0:T(8,128)(2,1)}) %reduce-scatter.7.cloned.1.call-update) | async-done | bytes 1048592 | tf_op jit(solution)/shard_map/reduce_scatter | solution.py:166
  508.8 72.9 %reduce-scatter.11.cloned.1.call-done = bf16[512,1024]{0,1:T(8,128)(2,1)} async-done(((bf16[4096,1024]{0,1:T(8,128)(2,1)}), bf16[512,1024]{0,1:T(8,128)(2,1)}) %reduce-scatter.11.cloned.1.call-update) | async-done | bytes 1048592 | tf_op jit(solution)/shard_map/reduce_scatter | solution.py:116
  584.9 157.7 %reduce-scatter.9.cloned.1.call-done = bf16[512,3072]{0,1:T(8,128)(2,1)} async-done(((bf16[4096,3072]{0,1:T(8,128)(2,1)}), bf16[512,3072]{0,1:T(8,128)(2,1)}) %reduce-scatter.9.cloned.1.call-update) | async-done | bytes 3145744 | tf_op jit(solution)/shard_map/reduce_scatter | solution.py:157
  742.6 5.4 copy.64
  748.0 9.5 %multiply_multiply_fusion = f32[512,3,1024]{2,0,1:T(8,128)} fusion(f32[512,3,1024]{2,0,1:T(8,128)} %copy.64, f32[512,3,1024]{2,0,1:T(8,128)} %reshape.76), kind=kLoop, calls=%fused_computation.8 | loop fusion | flops 3145728 | bytes 18874368 | tf_op jit(solution)/shard_map/mul | solution.py:165
  (89 shorter events, 56.5 us)
Async XLA Ops:
  7.2 138.3 %all-gather.7.cloned.1.call-start = ((), (), s32[]{:S(2)}) async-start(), calls=%async_computation.4 | async-start | bytes 5242880 | tf_op jit(solution)/shard_map/all_gather | solution.py:78
  7.9 188.2 %all-gather.11.cloned.1.call-start = ((), (), s32[]{:S(2)}) async-start(), calls=%async_computation.10 | async-start | bytes 2359296 | tf_op jit(solution)/shard_map/all_gather | solution.py:16
  86.4 33.6 %copy-start.11 = (s32[512,8]{0,1:T(8,128)S(1)}, s32[512,8]{0,1:T(8,128)}, u32[]{:S(2)}) copy-start(s32[512,8]{0,1:T(8,128)} %param.13) | copy-start | bytes 49156
  86.4 33.6 %copy-start.12 = (s32[512,8]{0,1:T(8,128)S(1)}, s32[512,8]{0,1:T(8,128)}, u32[]{:S(2)}) copy-start(s32[512,8]{0,1:T(8,128)} %param.14) | copy-start | bytes 49156
  163.6 3.9 copy-start.1
  163.6 2.3 copy-start.13
  165.2 113.3 %all-gather.9.cloned.1.call-start = ((), (), s32[]{:S(2)}) async-start(), calls=%async_computation.6 | async-start | bytes 5242880 | tf_op jit(solution)/shard_map/all_gather | solution.py:109
  165.9 233.5 %all-gather.13.cloned.1.call-start = ((), (), s32[]{:S(2)}) async-start(), calls=%async_computation.11 | async-start | bytes 2359296 | tf_op jit(solution)/shard_map/all_gather | solution.py:29
  167.5 2.0 copy-start.4
  199.4 80.2 %copy-start.3 = (f32[8,128,512]{2,1,0:T(8,128)}, f32[8,128,512]{2,1,0:T(8,128)S(1)}, u32[]{:S(2)}) copy-start(f32[8,128,512]{2,1,0:T(8,128)S(1)} %get-tuple-element.108) | copy-start | bytes 6291460
  279.6 12.4 %copy-start = (bf16[8,128,32,128]{3,2,1,0:T(8,128)(2,1)}, bf16[8,128,32,128]{3,2,1,0:T(8,128)(2,1)S(1)}, u32[]{:S(2)}) copy-start(bf16[8,128,32,128]{3,2,1,0:T(8,128)(2,1)S(1)} %mul.121) | copy-start | bytes 25165828
  298.3 175.6 %reduce-scatter.5.cloned.1.call-start = ((), (), s32[]{:S(2)}) async-start(), calls=%async_computation.5 | async-start | bytes 5242880 | tf_op jit(solution)/shard_map/reduce_scatter | solution.py:102
  312.3 194.1 %reduce-scatter.7.cloned.1.call-start = ((), (), s32[]{:S(2)}) async-start(), calls=%async_computation.7 | async-start | bytes 5242880 | tf_op jit(solution)/shard_map/reduce_scatter | solution.py:166
  387.4 2.7 copy-start.2
  394.5 2.9 copy-start.5
  407.3 3.2 copy-start.6
  410.5 2.5 copy-start.9
  432.8 148.8 %reduce-scatter.11.cloned.1.call-start = ((), (), s32[]{:S(2)}) async-start(), calls=%async_computation.9 | async-start | bytes 9437184 | tf_op jit(solution)/shard_map/reduce_scatter | solution.py:116
  443.5 299.1 %reduce-scatter.9.cloned.1.call-start = ((), (), s32[]{:S(2)}) async-start(), calls=%async_computation.8 | async-start | bytes 28311552 | tf_op jit(solution)/shard_map/reduce_scatter | solution.py:157
  462.6 0.7 copy-start.10
  466.7 7.2 copy-start.14
  466.7 7.2 copy-start.7
  473.9 32.5 %copy-start.8 = (bf16[128,4096]{1,0:T(8,128)(2,1)S(1)}, bf16[128,4096]{1,0:T(8,128)(2,1)}, u32[]{:S(2)}) copy-start(bf16[128,4096]{1,0:T(8,128)(2,1)} %param.19) | copy-start | bytes 3145732
Sparse Core Ops, SparseCore 0:
  9.6 83.4 all-gather.6
  165.3 30.7 all-gather.10
  197.6 80.7 all-gather.8
  298.5 26.4 all-gather.12
  327.1 76.7 reduce-scatter.4
  432.9 73.3 reduce-scatter.6
  509.8 71.7 reduce-scatter.10
  585.7 156.8 reduce-scatter.8

commit v2 on v1

--- a/solution.py
+++ b/solution.py
@@ -3,12 +3,88 @@
 import jax
 import jax.numpy as jnp
 from jax import lax
+from jax.experimental import pallas as pl
+from jax.experimental.pallas import tpu as pltpu
 from jax.sharding import PartitionSpec as P
 
 BLOCK = 128
 
 
 EPSILON = 1e-05
+
+def _tile(n, choices=(1024, 512, 256, 128)):
+    for c in choices:
+        if n % c == 0:
+            return c
+    return n
+
+def _nn_kernel(a_ref, w_ref, m_ref, o_ref, acc_ref, wm_ref):
+    k = pl.program_id(1)
+    @pl.when(k == 0)
+    def _():
+        acc_ref[...] = jnp.zeros_like(acc_ref)
+    for g in range(w_ref.shape[0] // BLOCK):
+        rows = slice(g * BLOCK, (g + 1) * BLOCK)
+        wm_ref[rows, :] = w_ref[rows, :] * m_ref[g]
+    acc_ref[...] += jnp.dot(a_ref[...], wm_ref[...], preferred_element_type=jnp.float32)
+    @pl.when(k == pl.num_programs(1) - 1)
+    def _():
+        o_ref[...] = acc_ref[...].astype(o_ref.dtype)
+
+def _nt_kernel(a_ref, w_ref, m_ref, o_ref, acc_ref, wm_ref):
+    k = pl.program_id(1)
+    @pl.when(k == 0)
+    def _():
+        acc_ref[...] = jnp.zeros_like(acc_ref)
+    for g in range(w_ref.shape[0] // BLOCK):
+        rows = slice(g * BLOCK, (g + 1) * BLOCK)
+        wm_ref[rows, :] = w_ref[rows, :] * m_ref[g]
+    acc_ref[...] += lax.dot_general(a_ref[...], wm_ref[...], (((1,), (1,)), ((), ())), preferred_element_type=jnp.float32)
+    @pl.when(k == pl.num_programs(1) - 1)
+    def _():
+        o_ref[...] = acc_ref[...].astype(o_ref.dtype)
+
+def masked_matmul(a, w, mask, out_dtype, transpose_w):
+    m = a.shape[0]
+    rows, cols = w.shape
+    if transpose_w:
+        tr, tk = _tile(rows), _tile(cols)
+        grid = (rows // tr, cols // tk)
+        in_specs = [
+            pl.BlockSpec((m, tk), lambda i, k: (0, k)),
+            pl.BlockSpec((tr, tk), lambda i, k: (i, k)),
+            pl.BlockSpec((tr // BLOCK, 1, tk), lambda i, k: (i, 0, k)),
+        ]
+        out_spec = pl.BlockSpec((m, tr), lambda i, k: (0, i))
+        out_shape = jax.ShapeDtypeStruct((m, rows), out_dtype)
+        scratch = [pltpu.VMEM((m, tr), jnp.float32), pltpu.VMEM((tr, tk), w.dtype)]
+        kernel = _nt_kernel
+        n_out = rows
+    else:
+        tk, tn = _tile(rows), _tile(cols)
+        grid = (cols // tn, rows // tk)
+        in_specs = [
+            pl.BlockSpec((m, tk), lambda j, k: (0, k)),
+            pl.BlockSpec((tk, tn), lambda j, k: (k, j)),
+            pl.BlockSpec((tk // BLOCK, 1, tn), lambda j, k: (k, 0, j)),
+        ]
+        out_spec = pl.BlockSpec((m, tn), lambda j, k: (0, j))
+        out_shape = jax.ShapeDtypeStruct((m, cols), out_dtype)
+        scratch = [pltpu.VMEM((m, tn), jnp.float32), pltpu.VMEM((tk, tn), w.dtype)]
+        kernel = _nn_kernel
+        n_out = cols
+    flops = 2 * m * rows * cols
+    nbytes = a.size * a.dtype.itemsize * (grid[0]) + w.size * w.dtype.itemsize + m * n_out * jnp.dtype(out_dtype).itemsize
+    return pl.pallas_call(
+        kernel,
+        grid=grid,
+        in_specs=in_specs,
+        out_specs=out_spec,
+        out_shape=out_shape,
+        scratch_shapes=scratch,
+        compiler_params=pltpu.CompilerParams(dimension_semantics=("parallel", "arbitrary"), vmem_limit_bytes=48 * 1024 * 1024),
+        cost_estimate=pl.CostEstimate(flops=flops, bytes_accessed=nbytes, transcendentals=0),
+    )(a, w, mask)
 
 
 def carried_in(value, axis, join, neutral):
@@ -67,16 +143,15 @@
     col_blocks = features // BLOCK
     highest = lax.Precision.HIGHEST
     qkv_mask = jnp.transpose(qkv_blocks, (1, 0, 2)).astype(jnp.bfloat16)
-    qkv_used = (
-        qkv_weight.reshape(row_blocks, BLOCK, 3, col_blocks, BLOCK)
-        * qkv_mask[:, None, :, :, None]
-    ).reshape(model_width, 3 * features)
-    out_used = (
-        out_weight.reshape(col_blocks, BLOCK, row_blocks, BLOCK)
-        * out_blocks.astype(jnp.bfloat16)[:, None, :, None]
-    ).reshape(features, model_width)
+    qkv_flat = qkv_weight.reshape(model_width, 3 * features)
+    qkv_spread = jnp.broadcast_to(
+        qkv_mask[:, :, :, None], (row_blocks, 3, col_blocks, BLOCK)
+    ).reshape(row_blocks, 1, 3 * features)
+    out_spread = jnp.broadcast_to(
+        out_blocks.astype(jnp.bfloat16)[:, :, None], (col_blocks, row_blocks, BLOCK)
+    ).reshape(col_blocks, 1, model_width)
     gathered = lax.all_gather(tokens, "tp", axis=0, tiled=True)
-    projected = jnp.dot(gathered, qkv_used, preferred_element_type=jnp.float32).astype(jnp.bfloat16)
+    projected = masked_matmul(gathered, qkv_flat, qkv_spread, jnp.bfloat16, False)
     projected = projected.reshape(block_rows, 3, local_heads, head_width)
     query_spikes = spike_query.astype(jnp.bfloat16)[:, :, None]
     key_spikes = spike_key.astype(jnp.bfloat16)[:, :, None]
@@ -100,7 +175,7 @@
     normed = mixed_rows * inv_rms
     attended = normed.astype(jnp.bfloat16).reshape(block_rows, features)
     head_sum = lax.psum_scatter(
-        jnp.dot(attended, out_used, preferred_element_type=jnp.float32).astype(jnp.bfloat16),
+        masked_matmul(attended, out_weight, out_spread, jnp.bfloat16, False),
         "tp",
         scatter_dimension=0,
         tiled=True,
@@ -122,7 +197,7 @@
         (slice_blocks, BLOCK, col_blocks, BLOCK),
     ).reshape(slice_rows, features)
     out_grad = jnp.transpose(out_sum * out_keep * norm_factor)
-    grad_attended = jnp.einsum("tm,fm->tf", grad_rows, out_used, preferred_element_type=jnp.float32)
+    grad_attended = masked_matmul(grad_rows, out_weight, out_spread, jnp.float32, True)
     grad_attended = grad_attended.reshape(block_rows, local_heads, head_width)
     inner_mean = jnp.mean(grad_attended * normed, axis=-1, keepdims=True)
     grad_mixed = inv_rms * (grad_attended - normed * inner_mean)
@@ -164,9 +239,7 @@
     ).reshape(slice_rows, 3, features)
     qkv_grad = qkv_sum.reshape(slice_rows, 3, features) * qkv_keep * norm_factor
     token_sum = lax.psum_scatter(
-        jnp.einsum("tc,mc->tm", grad_proj, qkv_used, preferred_element_type=jnp.float32).astype(
-            jnp.bfloat16
-        ),
+        masked_matmul(grad_proj, qkv_flat, qkv_spread, jnp.bfloat16, True),
         "tp",
         scatter_dimension=0,
         tiled=True,

time: 775 us -> 665 us (0.86)
  local copies, waits for them, and re-layouts: 179 us -> 105 us
  matrix products: 122 us -> 57.3 us
  Pallas kernels: 0 us -> 59.1 us
  other arithmetic: 83.5 us -> 27.8 us
  waiting for transfers between devices: 365 us -> 397 us
    mul x6 -> x0, local copies, waits for them, and re-layouts: 125 us -> none  [the longest x5 124 us: on_device(): qkv_weight.reshape(row_blocks, BLOCK, 3, col_blocks, BLOCK)]
    dot_general x4 -> x0, matrix products: 63.5 us -> none  [the longest x1 19.5 us: on_device(): jnp.einsum('tc,mc->tm', grad_proj, qkv_used, preferred_element_type=jnp.f...]
    pallas_call x0 -> x4, Pallas kernels: none -> 59.1 us  [masked_matmul(): pl.pallas_call(kernel, grid=grid, in_specs=in_specs, out_specs=out_spec,...]
    mul x2 -> x0, other arithmetic: 54.1 us -> none  [on_device(): qkv_weight.reshape(row_blocks, BLOCK, 3, col_blocks, BLOCK)]
    reduce_scatter x2, waiting for transfers between devices: 29.9 us -> 73.6 us  [the longest x1 73.6 us: on_device(): lax.psum_scatter(masked_matmul(grad_proj, qkv_flat, qkv_spread, jnp.bfloa...]
    reshape x0 -> x6, local copies, waits for them, and re-layouts: none -> 38.4 us  [the longest x1 32.8 us: on_device(): qkv_flat = qkv_weight.reshape(model_width, 3 * features)]
    all_gather x1, waiting for transfers between devices: 79 us -> 53.4 us  [on_device(): grad_rows = lax.all_gather(cotangent, 'tp', axis=0, tiled=True)]
    all_gather x1, waiting for transfers between devices: 0.01 us -> 17.2 us  [on_device(): gathered = lax.all_gather(tokens, 'tp', axis=0, tiled=True)]
  transfers between devices with their start and end apart: 8 -> 8, of which waited for: 5 -> 7; matrix products, arithmetic and copies ran while one was open for 43% -> 24% of each run, Pallas kernels for 0% -> 9%
where the time goes in v2:
time: 665 us; the launch traced here: 662 us
  waiting for transfers between devices  397 us (60%)
  local copies, waits for them, and re-layouts  105 us (16%)
  Pallas kernels  59.1 us (9%)
  matrix products  57.3 us (9%)
  other arithmetic  27.8 us (4%)
  between operations  14.6 us (2%)
    reduce_scatter x1, waiting for transfers between devices, on_device(): lax.psum_scatter(qkv_part.astype(jnp.bfloat16), 'ctx', scatter_dimension=...  158 us
    reduce_scatter x1, waiting for transfers between devices, on_device(): lax.psum_scatter(masked_matmul(grad_proj, qkv_flat, qkv_spread, jnp.bfloa...  73.6 us
    reduce_scatter x1, waiting for transfers between devices, on_device(): lax.psum_scatter(out_part.astype(jnp.bfloat16), 'ctx', scatter_dimension=...  72.8 us
    pallas_call x4, Pallas kernels, masked_matmul(): pl.pallas_call(kernel, grid=grid, in_specs=in_specs, out_specs=out_spec,...  59.1 us
    all_gather x1, waiting for transfers between devices, on_device(): grad_rows = lax.all_gather(cotangent, 'tp', axis=0, tiled=True)  53.4 us
    unnamed x66, local copies, waits for them, and re-layouts  48.5 us
    reshape x1, local copies, waits for them, and re-layouts, on_device(): qkv_flat = qkv_weight.reshape(model_width, 3 * features)  32.8 us
    dot_general x1, matrix products, on_device(): jnp.einsum('tm,tc->mc', gathered, grad_proj, preferred_element_type=jnp.f...  19 us
  transfers between devices with their start and end apart: 8, of which 7 were waited for; matrix products, arithmetic and copies ran while one was open for 24% of the time, Pallas kernels for 9%

profile of v2, /device:TPU:0, one launch (start us, length us, event | category | flops | bytes accessed | tf_op | source)
XLA Modules:
  0.0 662.1 jit_solution(16887706942785163251)
XLA Ops:
  8.7 33.4 %copy.64 = bf16[4096,3,1024]{0,2,1:T(8,128)(2,1)} copy(bf16[4096,3,1024]{2,0,1:T(8,128)(2,1)} %param.15) | data formatting | bytes 50331648 | tf_op args[3]
  42.1 32.8 %copy.66.w_ref = bf16[4096,3072]{1,0:T(8,128)(2,1)} copy(bf16[4096,3072]{0,1:T(8,128)(2,1)} %bitcast.121) | data formatting | bytes 50331648 | tf_op jit(solution)/shard_map/reshape | solution.py:146
  75.9 17.2 %all-gather.7.cloned.1.call-done.a_ref = bf16[512,4096]{1,0:T(8,128)(2,1)} async-done(((bf16[128,4096]{1,0:T(8,128)(2,1)}), bf16[512,4096]{1,0:T(8,128)(2,1)}) %all-gather.7.cloned.1.call-update) | async-done | bytes 4194320 | tf_op jit(solution)/shard_map/all_gather | solution.py:153
  93.1 22.0 %shard_map.111 = bf16[512,3072]{1,0:T(8,128)(2,1)S(1)} custom-call(bf16[512,4096]{1,0:T(8,128)(2,1)} %all-gather.7.cloned.1.call-done.a_ref, bf16[4096,3072]{1,0:T(8,128)(2,1)} %copy.66.w_ref, bf16[32,1,3072]{2,1,0:T(2,128)(2,1)S(1)} %reshape.84.m_ref), custom_call_target="tpu_custom_call" | custom-call | flops 12884901888 | bytes 40894464 | tf_op jit(solution)/shard_map/pallas_call | solution.py:78
  120.6 53.4 %all-gather.9.cloned.1.call-done.a_ref = bf16[512,4096]{1,0:T(8,128)(2,1)} async-done(((bf16[128,4096]{1,0:T(8,128)(2,1)}), bf16[512,4096]{1,0:T(8,128)(2,1)}) %all-gather.9.cloned.1.call-update) | async-done | bytes 4194320 | tf_op jit(solution)/shard_map/all_gather | solution.py:184
  174.0 8.2 %shard_map.113 = f32[512,1024]{1,0:T(8,128)S(1)} custom-call(bf16[512,4096]{1,0:T(8,128)(2,1)} %all-gather.9.cloned.1.call-done.a_ref, bf16[1024,4096]{1,0:T(8,128)(2,1)} %w_ref.3, bf16[8,1,4096]{2,1,0:T(2,128)(2,1)S(1)} %reshape.85.m_ref), custom_call_target="tpu_custom_call" | custom-call | flops 4294967296 | bytes 14680064 | tf_op jit(solution)/shard_map/pallas_call | solution.py:78
  192.7 9.6 %all-gather.11.cloned.1.call-done = bf16[64,128,128]{2,1,0:T(8,128)(2,1)} async-done(((bf16[8,128,128]{2,1,0:T(8,128)(2,1)}), bf16[64,128,128]{2,1,0:T(8,128)(2,1)}) %all-gather.11.cloned.1.call-update) | async-done | bytes 2097168 | tf_op jit(solution)/shard_map/all_gather | solution.py:92
  202.6 2.9 fusion.4
  210.6 7.2 %shard_map.112 = bf16[512,4096]{1,0:T(8,128)(2,1)S(1)} custom-call(bf16[512,1024]{1,0:T(8,128)(2,1)S(1)} %copy.105.a_ref, bf16[1024,4096]{1,0:T(8,128)(2,1)} %w_ref.3, bf16[8,1,4096]{2,1,0:T(2,128)(2,1)S(1)} %reshape.85.m_ref), custom_call_target="tpu_custom_call" | custom-call | flops 4294967296 | bytes 16777216 | tf_op jit(solution)/shard_map/pallas_call | solution.py:78
  226.8 3.0 fusion.7
  234.7 10.8 %all-gather.13.cloned.1.call-done = bf16[64,128,128]{2,1,0:T(8,128)(2,1)} async-done(((bf16[8,128,128]{2,1,0:T(8,128)(2,1)}), bf16[64,128,128]{2,1,0:T(8,128)(2,1)}) %all-gather.13.cloned.1.call-update) | async-done | bytes 2097168 | tf_op jit(solution)/shard_map/all_gather | solution.py:105
  245.6 8.0 %while.23 = (s32[]{:T(128)}, f32[8,128,128]{2,1,0:T(8,128)S(1)}, s32[]{:T(128)}, bf16[8,8,128,128]{3,2,1,0:T(8,128)(2,1)}, s32[]{:T(128)}, /*index=5*/s32[]{:T(128)}, s32[]{:T(128)}, s32[]{:T(128)}) while((s32[]{:T(128)}, f32[8,128,128]{2,1,0:T(8,128)S(1)}, s32[]{:T(128)}, bf16[8,8,128,128]{3,2,1,0:T(8,128)(2,1)}, s32[]{:T(128)}, ...), condition=%wide.region_6.7_spmd, body=%wide.region_5.6_spmd.sunk | while | flops 262150 | bytes 1310863 | solution.py:114
  253.6 3.0 fusion.8
  260.7 3.2 copy.106.a_ref
  263.9 21.6 %shard_map.114 = bf16[512,4096]{1,0:T(8,128)(2,1)} custom-call(bf16[512,3072]{1,0:T(8,128)(2,1)S(1)} %copy.106.a_ref, bf16[4096,3072]{1,0:T(8,128)(2,1)} %copy.66.w_ref, bf16[32,1,3072]{2,1,0:T(2,128)(2,1)S(1)} %reshape.84.m_ref), custom_call_target="tpu_custom_call" | custom-call | flops 12884901888 | bytes 41943040 | tf_op jit(solution)/shard_map/pallas_call | solution.py:78
  286.8 8.9 %convert_bitcast_fusion.1 = bf16[4096,1024]{0,1:T(8,128)(2,1)} fusion(bf16[512,1024]{0,1:T(8,128)(2,1)S(1)} %bitcast.128, bf16[512,4096]{1,0:T(8,128)(2,1)} %all-gather.9.cloned.1.call-done.a_ref), kind=kOutput, calls=%fused_computation.3 | convolution fusion | flops 4299161600 | bytes 13631488 | tf_op jit(solution)/shard_map/tm,tf->mf/dot_general | solution.py:190
  297.6 19.0 %convert_bitcast_fusion = bf16[4096,3072]{0,1:T(8,128)(2,1)} fusion(bf16[512,3072]{0,1:T(8,128)(2,1)S(1)} %bitcast.124, bf16[512,4096]{1,0:T(8,128)(2,1)} %all-gather.7.cloned.1.call-done.a_ref), kind=kOutput, calls=%fused_computation.2 | convolution fusion | flops 12897484800 | bytes 32505856 | tf_op jit(solution)/shard_map/tm,tc->mc/dot_general | solution.py:231
  317.5 3.2 broadcast_in_dim.50
  320.7 7.1 %reshape.76 = f32[512,3,1024]{2,0,1:T(8,128)} reshape(f32[4,128,3,8,128]{4,3,1,0,2:T(8,128)} %broadcast_in_dim.50) | data formatting | bytes 12582912 | tf_op jit(solution)/shard_map/reshape | solution.py:239
  330.5 73.6 %reduce-scatter.7.cloned.1.call-done = bf16[128,4096]{1,0:T(8,128)(2,1)} async-done(((bf16[512,4096]{1,0:T(8,128)(2,1)}), bf16[128,4096]{1,0:T(8,128)(2,1)}) %reduce-scatter.7.cloned.1.call-update) | async-done | bytes 1048592 | tf_op jit(solution)/shard_map/reduce_scatter | solution.py:241
  406.5 72.8 %reduce-scatter.11.cloned.1.call-done = bf16[512,1024]{0,1:T(8,128)(2,1)} async-done(((bf16[4096,1024]{0,1:T(8,128)(2,1)}), bf16[512,1024]{0,1:T(8,128)(2,1)}) %reduce-scatter.11.cloned.1.call-update) | async-done | bytes 1048592 | tf_op jit(solution)/shard_map/reduce_scatter | solution.py:191
  482.3 158.1 %reduce-scatter.9.cloned.1.call-done = bf16[512,3072]{0,1:T(8,128)(2,1)} async-done(((bf16[4096,3072]{0,1:T(8,128)(2,1)}), bf16[512,3072]{0,1:T(8,128)(2,1)}) %reduce-scatter.9.cloned.1.call-update) | async-done | bytes 3145744 | tf_op jit(solution)/shard_map/reduce_scatter | solution.py:232
  640.3 5.4 copy.92
  645.7 9.5 %multiply_multiply_fusion = f32[512,3,1024]{2,0,1:T(8,128)} fusion(f32[512,3,1024]{2,0,1:T(8,128)} %copy.92, f32[512,3,1024]{2,0,1:T(8,128)} %reshape.76), kind=kLoop, calls=%fused_computation.6 | loop fusion | flops 3145728 | bytes 18874368 | tf_op jit(solution)/shard_map/mul | solution.py:240
  (126 shorter events, 61.0 us)
Async XLA Ops:
  7.2 85.9 %all-gather.7.cloned.1.call-start = ((), (), s32[]{:S(2)}) async-start(), calls=%async_computation.4 | async-start | bytes 5242880 | tf_op jit(solution)/shard_map/all_gather | solution.py:153
  7.9 166.1 %all-gather.9.cloned.1.call-start = ((), (), s32[]{:S(2)}) async-start(), calls=%async_computation.6 | async-start | bytes 5242880 | tf_op jit(solution)/shard_map/all_gather | solution.py:184
  8.6 193.7 %all-gather.11.cloned.1.call-start = ((), (), s32[]{:S(2)}) async-start(), calls=%async_computation.10 | async-start | bytes 2359296 | tf_op jit(solution)/shard_map/all_gather | solution.py:92
  42.1 32.8 %copy-start.25 = (s32[3,32,8]{1,2,0:T(8,128)S(1)}, s32[3,32,8]{1,2,0:T(8,128)}, u32[]{:S(2)}) copy-start(s32[3,32,8]{1,2,0:T(8,128)} %param.16) | copy-start | bytes 9220
  42.1 33.1 %copy-start.27 = (s32[512,8]{0,1:T(8,128)S(1)}, s32[512,8]{0,1:T(8,128)}, u32[]{:S(2)}) copy-start(s32[512,8]{0,1:T(8,128)} %param.13) | copy-start | bytes 49156
  42.1 33.1 %copy-start.28 = (s32[512,8]{0,1:T(8,128)S(1)}, s32[512,8]{0,1:T(8,128)}, u32[]{:S(2)}) copy-start(s32[512,8]{0,1:T(8,128)} %param.14) | copy-start | bytes 49156
  120.2 125.3 %all-gather.13.cloned.1.call-start = ((), (), s32[]{:S(2)}) async-start(), calls=%async_computation.11 | async-start | bytes 2359296 | tf_op jit(solution)/shard_map/all_gather | solution.py:105
  185.7 21.0 %copy-start.6 = (bf16[512,1,8,128]{0,3,2,1:T(8,128)(2,1)}, bf16[512,1,8,128]{0,3,2,1:T(8,128)(2,1)S(1)}, u32[]{:S(2)}) copy-start(bf16[512,1,8,128]{0,3,2,1:T(8,128)(2,1)S(1)} %copy.109) | copy-start | bytes 3145732
  185.7 4.1 copy-start.9
  202.5 2.9 copy-start.3
  206.7 3.9 copy-start.19
  210.0 118.0 %reduce-scatter.5.cloned.1.call-start = ((), (), s32[]{:S(2)}) async-start(), calls=%async_computation.5 | async-start | bytes 5242880 | tf_op jit(solution)/shard_map/reduce_scatter | solution.py:177
  219.9 184.2 %reduce-scatter.7.cloned.1.call-start = ((), (), s32[]{:S(2)}) async-start(), calls=%async_computation.7 | async-start | bytes 5242880 | tf_op jit(solution)/shard_map/reduce_scatter | solution.py:241
  226.8 3.0 copy-start.7
  229.7 2.9 copy-start.5
  245.6 8.0 %copy-start.10 = (bf16[512,1,8,128]{0,3,2,1:T(8,128)(2,1)S(1)}, bf16[512,1,8,128]{0,3,2,1:T(8,128)(2,1)}, u32[]{:S(2)}) copy-start(bf16[512,1,8,128]{0,3,2,1:T(8,128)(2,1)} %copy-done.8) | copy-start | bytes 3145732
  245.6 8.0 %copy-start.23 = (f32[512,8]{0,1:T(8,128)S(1)}, f32[512,8]{0,1:T(8,128)}, u32[]{:S(2)}) copy-start(f32[512,8]{0,1:T(8,128)} %get-tuple-element.112) | copy-start | bytes 49156
  253.6 3.1 copy-start.15
  253.6 3.1 copy-start.16
  285.6 193.7 %reduce-scatter.11.cloned.1.call-start = ((), (), s32[]{:S(2)}) async-start(), calls=%async_computation.9 | async-start | bytes 9437184 | tf_op jit(solution)/shard_map/reduce_scatter | solution.py:191
  295.7 344.6 %reduce-scatter.9.cloned.1.call-start = ((), (), s32[]{:S(2)}) async-start(), calls=%async_computation.8 | async-start | bytes 28311552 | tf_op jit(solution)/shard_map/reduce_scatter | solution.py:232
  320.7 7.2 %copy-start.30 = (s32[8,32]{1,0:T(8,128)S(1)}, s32[8,32]{1,0:T(8,128)}, u32[]{:S(2)}) copy-start(s32[8,32]{1,0:T(8,128)} %param.18) | copy-start | bytes 3076
  320.7 7.2 %copy-start.17 = (bf16[128,4096]{1,0:T(8,128)(2,1)S(1)}, bf16[128,4096]{1,0:T(8,128)(2,1)}, u32[]{:S(2)}) copy-start(bf16[128,4096]{1,0:T(8,128)(2,1)} %param.12) | copy-start | bytes 3145732
  327.9 76.2 %copy-start.18 = (bf16[128,4096]{1,0:T(8,128)(2,1)S(1)}, bf16[128,4096]{1,0:T(8,128)(2,1)}, u32[]{:S(2)}) copy-start(bf16[128,4096]{1,0:T(8,128)(2,1)} %param.19) | copy-start | bytes 3145732
  (15 other events, 28.1 us)
Sparse Core Ops, SparseCore 0:
  9.6 83.4 all-gather.6
  94.6 79.2 all-gather.8
  175.8 26.4 all-gather.10
  210.1 35.4 all-gather.12
  247.7 76.7 reduce-scatter.4
  326.8 77.2 reduce-scatter.6
  407.5 71.7 reduce-scatter.10
  483.4 156.8 reduce-scatter.8

commit v3 on v1

--- a/solution.py
+++ b/solution.py
@@ -3,12 +3,117 @@
 import jax
 import jax.numpy as jnp
 from jax import lax
+from jax.experimental import pallas as pl
+from jax.experimental.pallas import tpu as pltpu
 from jax.sharding import PartitionSpec as P
 
 BLOCK = 128
 
 
 EPSILON = 1e-05
+
+def _tile(n, choices=(1024, 512, 256, 128)):
+    for c in choices:
+        if n % c == 0:
+            return c
+    return n
+
+
+def _masked_tile(w_ref, m_ref, wm_ref):
+    for g in range(w_ref.shape[0] // BLOCK):
+        rows = slice(g * BLOCK, (g + 1) * BLOCK)
+        wm_ref[rows, :] = w_ref[rows, :] * m_ref[g]
+
+
+def _nn_kernel(a_ref, w_ref, m_ref, o_ref, acc_ref, wm_ref):
+    k = pl.program_id(2)
+
+    @pl.when(k == 0)
+    def _():
+        acc_ref[...] = jnp.zeros_like(acc_ref)
+
+    _masked_tile(w_ref, m_ref, wm_ref)
+    acc_ref[...] += jnp.dot(a_ref[...], wm_ref[...], preferred_element_type=jnp.float32)
+
+    @pl.when(k == pl.num_programs(2) - 1)
+    def _():
+        o_ref[...] = acc_ref[...].astype(o_ref.dtype)
+
+
+def _nt_kernel(a_ref, w_ref, m_ref, o_ref, acc_ref, wm_ref):
+    p = pl.program_id(1)
+    k = pl.program_id(2)
+
+    @pl.when((p == 0) & (k == 0))
+    def _():
+        acc_ref[...] = jnp.zeros_like(acc_ref)
+
+    _masked_tile(w_ref, m_ref, wm_ref)
+    acc_ref[...] += lax.dot_general(
+        a_ref[...], wm_ref[...], (((1,), (1,)), ((), ())), preferred_element_type=jnp.float32
+    )
+
+    @pl.when((p == pl.num_programs(1) - 1) & (k == pl.num_programs(2) - 1))
+    def _():
+        o_ref[...] = acc_ref[...].astype(o_ref.dtype)
+
+
+def masked_matmul_nn(a, w, mask, out_dtype):
+    m = a.shape[0]
+    planes, rows, cols = w.shape
+    tk, tn = _tile(rows), _tile(cols)
+    grid = (planes, cols // tn, rows // tk)
+    return pl.pallas_call(
+        _nn_kernel,
+        grid=grid,
+        in_specs=[
+            pl.BlockSpec((m, tk), lambda p, j, k: (0, k)),
+            pl.BlockSpec((None, tk, tn), lambda p, j, k: (p, k, j)),
+            pl.BlockSpec((None, tk // BLOCK, 1, tn), lambda p, j, k: (p, k, 0, j)),
+        ],
+        out_specs=pl.BlockSpec((None, m, tn), lambda p, j, k: (p, 0, j)),
+        out_shape=jax.ShapeDtypeStruct((planes, m, cols), out_dtype),
+        scratch_shapes=[pltpu.VMEM((m, tn), jnp.float32), pltpu.VMEM((tk, tn), w.dtype)],
+        compiler_params=pltpu.CompilerParams(
+            dimension_semantics=("parallel", "parallel", "arbitrary"),
+            vmem_limit_bytes=48 * 1024 * 1024,
+        ),
+        cost_estimate=pl.CostEstimate(
+            flops=2 * m * planes * rows * cols,
+            bytes_accessed=a.size * 2 * planes * (cols // tn) + w.size * 2
+            + m * planes * cols * jnp.dtype(out_dtype).itemsize,
+            transcendentals=0,
+        ),
+    )(a, w, mask)
+
+
+def masked_matmul_nt(a, w, mask, out_dtype):
+    planes, m, _ = a.shape
+    _, rows, cols = w.shape
+    tr, tk = _tile(rows), _tile(cols)
+    grid = (rows // tr, planes, cols // tk)
+    return pl.pallas_call(
+        _nt_kernel,
+        grid=grid,
+        in_specs=[
+            pl.BlockSpec((None, m, tk), lambda i, p, k: (p, 0, k)),
+            pl.BlockSpec((None, tr, tk), lambda i, p, k: (p, i, k)),
+            pl.BlockSpec((None, tr // BLOCK, 1, tk), lambda i, p, k: (p, i, 0, k)),
+        ],
+        out_specs=pl.BlockSpec((m, tr), lambda i, p, k: (0, i)),
+        out_shape=jax.ShapeDtypeStruct((m, rows), out_dtype),
+        scratch_shapes=[pltpu.VMEM((m, tr), jnp.float32), pltpu.VMEM((tr, tk), w.dtype)],
+        compiler_params=pltpu.CompilerParams(
+            dimension_semantics=("parallel", "arbitrary", "arbitrary"),
+            vmem_limit_bytes=48 * 1024 * 1024,
+        ),
+        cost_estimate=pl.CostEstimate(
+            flops=2 * m * planes * rows * cols,
+            bytes_accessed=a.size * 2 * (rows // tr) + w.size * 2
+            + m * rows * jnp.dtype(out_dtype).itemsize,
+            transcendentals=0,
+        ),
+    )(a, w, mask)
 
 
 def carried_in(value, axis, join, neutral):
@@ -66,23 +171,24 @@
     row_blocks = model_width // BLOCK
     col_blocks = features // BLOCK
     highest = lax.Precision.HIGHEST
-    qkv_mask = jnp.transpose(qkv_blocks, (1, 0, 2)).astype(jnp.bfloat16)
-    qkv_used = (
-        qkv_weight.reshape(row_blocks, BLOCK, 3, col_blocks, BLOCK)
-        * qkv_mask[:, None, :, :, None]
-    ).reshape(model_width, 3 * features)
-    out_used = (
-        out_weight.reshape(col_blocks, BLOCK, row_blocks, BLOCK)
-        * out_blocks.astype(jnp.bfloat16)[:, None, :, None]
-    ).reshape(features, model_width)
+    qkv_planes = jnp.transpose(qkv_weight, (1, 0, 2))
+    qkv_spread = jnp.broadcast_to(
+        qkv_blocks.astype(jnp.bfloat16)[:, :, None, :, None],
+        (3, row_blocks, 1, col_blocks, BLOCK),
+    ).reshape(3, row_blocks, 1, features)
+    out_planes = out_weight[None]
+    out_spread = jnp.broadcast_to(
+        out_blocks.astype(jnp.bfloat16)[None, :, None, :, None],
+        (1, col_blocks, 1, row_blocks, BLOCK),
+    ).reshape(1, col_blocks, 1, model_width)
     gathered = lax.all_gather(tokens, "tp", axis=0, tiled=True)
-    projected = jnp.dot(gathered, qkv_used, preferred_element_type=jnp.float32).astype(jnp.bfloat16)
-    projected = projected.reshape(block_rows, 3, local_heads, head_width)
+    projected = masked_matmul_nn(gathered, qkv_planes, qkv_spread, jnp.bfloat16)
+    projected = projected.reshape(3, block_rows, local_heads, head_width)
     query_spikes = spike_query.astype(jnp.bfloat16)[:, :, None]
     key_spikes = spike_key.astype(jnp.bfloat16)[:, :, None]
-    query_spiked = projected[:, 0] * query_spikes
-    key_spiked = projected[:, 1] * key_spikes
-    values = projected[:, 2]
+    query_spiked = projected[0] * query_spikes
+    key_spiked = projected[1] * key_spikes
+    values = projected[2]
     query_wide = query_spiked.astype(jnp.float32)
     key_wide = key_spiked.astype(jnp.float32)
     local_state = jnp.einsum("shd,she->hde", key_spiked, values, preferred_element_type=jnp.float32)
@@ -100,7 +206,7 @@
     normed = mixed_rows * inv_rms
     attended = normed.astype(jnp.bfloat16).reshape(block_rows, features)
     head_sum = lax.psum_scatter(
-        jnp.dot(attended, out_used, preferred_element_type=jnp.float32).astype(jnp.bfloat16),
+        masked_matmul_nn(attended, out_planes, out_spread, jnp.bfloat16)[0],
         "tp",
         scatter_dimension=0,
         tiled=True,
@@ -122,7 +228,7 @@
         (slice_blocks, BLOCK, col_blocks, BLOCK),
     ).reshape(slice_rows, features)
     out_grad = jnp.transpose(out_sum * out_keep * norm_factor)
-    grad_attended = jnp.einsum("tm,fm->tf", grad_rows, out_used, preferred_element_type=jnp.float32)
+    grad_attended = masked_matmul_nt(grad_rows[None], out_planes, out_spread, jnp.float32)
     grad_attended = grad_attended.reshape(block_rows, local_heads, head_width)
     inner_mean = jnp.mean(grad_attended * normed, axis=-1, keepdims=True)
     grad_mixed = inv_rms * (grad_attended - normed * inner_mean)
@@ -151,22 +257,20 @@
             (grad_key * key_spikes.astype(jnp.float32)).astype(jnp.bfloat16),
             grad_value.astype(jnp.bfloat16),
         ],
-        axis=1,
-    ).reshape(block_rows, 3 * features)
-    qkv_part = jnp.einsum("tm,tc->mc", gathered, grad_proj, preferred_element_type=jnp.float32)
+        axis=0,
+    ).reshape(3, block_rows, features)
+    qkv_part = jnp.einsum("tm,ptc->mpc", gathered, grad_proj, preferred_element_type=jnp.float32)
     qkv_sum = lax.psum_scatter(
         qkv_part.astype(jnp.bfloat16), "ctx", scatter_dimension=0, tiled=True
     ).astype(jnp.float32)
-    qkv_keep = lax.dynamic_slice_in_dim(qkv_mask, ctx_place * slice_blocks, slice_blocks, 0)
+    qkv_keep = lax.dynamic_slice_in_dim(qkv_blocks, ctx_place * slice_blocks, slice_blocks, 1)
     qkv_keep = jnp.broadcast_to(
-        qkv_keep.astype(jnp.float32)[:, None, :, :, None],
+        jnp.transpose(qkv_keep, (1, 0, 2)).astype(jnp.float32)[:, None, :, :, None],
         (slice_blocks, BLOCK, 3, col_blocks, BLOCK),
     ).reshape(slice_rows, 3, features)
-    qkv_grad = qkv_sum.reshape(slice_rows, 3, features) * qkv_keep * norm_factor
+    qkv_grad = qkv_sum * qkv_keep * norm_factor
     token_sum = lax.psum_scatter(
-        jnp.einsum("tc,mc->tm", grad_proj, qkv_used, preferred_element_type=jnp.float32).astype(
-            jnp.bfloat16
-        ),
+        masked_matmul_nt(grad_proj, qkv_planes, qkv_spread, jnp.bfloat16),
         "tp",
         scatter_dimension=0,
         tiled=True,

time: 775 us -> 663 us (0.86); the launches traced: 765 us -> 661 us
  local copies, waits for them, and re-layouts: 179 us -> 42.4 us
  waiting for transfers between devices: 365 us -> 455 us
  other arithmetic: 83.5 us -> 23.4 us
  Pallas kernels: 0 us -> 58.5 us
  matrix products: 122 us -> 66 us
    mul x6 -> x0, local copies, waits for them, and re-layouts: 125 us -> none  [the longest x5 124 us: on_device(): qkv_weight.reshape(row_blocks, BLOCK, 3, col_blocks, BLOCK)]
    all_gather x1, waiting for transfers between devices: 0.01 us -> 84 us  [on_device(): gathered = lax.all_gather(tokens, 'tp', axis=0, tiled=True)]
    dot_general x5 -> x1, matrix products: 82.6 us -> 20.7 us  [on_device(): jnp.einsum('tm,ptc->mpc', gathered, grad_proj, preferred_element_type=jnp...]
    pallas_call x0 -> x4, Pallas kernels: none -> 58.5 us  [the longest x2 29.5 us: masked_matmul_nt(): pl.pallas_call(_nt_kernel, grid=grid, in_specs=[pl.BlockSpec((None, m, tk...]
    mul x3 -> x1, other arithmetic: 63.7 us -> 7.4 us  [on_device(): qkv_grad = qkv_sum * qkv_keep * norm_factor]
    reduce_scatter x2, waiting for transfers between devices: 29.9 us -> 70.1 us  [the longest x1 70.1 us: on_device(): lax.psum_scatter(masked_matmul_nt(grad_proj, qkv_planes, qkv_spread, jnp....]
    all_gather x1, waiting for transfers between devices: 79 us -> 53.1 us  [on_device(): grad_rows = lax.all_gather(cotangent, 'tp', axis=0, tiled=True)]
    unnamed x31 -> x58, local copies, waits for them, and re-layouts: 37.1 us -> 20.9 us
  transfers between devices with their start and end apart: 8 -> 8, of which waited for: 5 -> 7; matrix products, arithmetic and copies ran while one was open for 43% -> 15% of each run, Pallas kernels for 0% -> 9%
where the time goes in v3:
time: 663 us; the launch traced here: 661 us
  waiting for transfers between devices  455 us (69%)
  matrix products  66 us (10%)
  Pallas kernels  58.5 us (9%)
  local copies, waits for them, and re-layouts  42.4 us (6%)
  other arithmetic  23.4 us (4%)
  between operations  14.6 us (2%)
    reduce_scatter x1, waiting for transfers between devices, on_device(): lax.psum_scatter(qkv_part.astype(jnp.bfloat16), 'ctx', scatter_dimension=...  158 us
    all_gather x1, waiting for transfers between devices, on_device(): gathered = lax.all_gather(tokens, 'tp', axis=0, tiled=True)  84 us
    reduce_scatter x1, waiting for transfers between devices, on_device(): lax.psum_scatter(out_part.astype(jnp.bfloat16), 'ctx', scatter_dimension=...  72.8 us
    reduce_scatter x1, waiting for transfers between devices, on_device(): lax.psum_scatter(masked_matmul_nt(grad_proj, qkv_planes, qkv_spread, jnp....  70.1 us
    all_gather x1, waiting for transfers between devices, on_device(): grad_rows = lax.all_gather(cotangent, 'tp', axis=0, tiled=True)  53.1 us
    pallas_call x2, Pallas kernels, masked_matmul_nt(): pl.pallas_call(_nt_kernel, grid=grid, in_specs=[pl.BlockSpec((None, m, tk...  29.5 us
    pallas_call x2, Pallas kernels, masked_matmul_nn(): pl.pallas_call(_nn_kernel, grid=grid, in_specs=[pl.BlockSpec((m, tk), lam...  29 us
    unnamed x58, local copies, waits for them, and re-layouts  20.9 us
  transfers between devices with their start and end apart: 8, of which 7 were waited for; matrix products, arithmetic and copies ran while one was open for 15% of the time, Pallas kernels for 9%

profile of v3, /device:TPU:0, one launch (start us, length us, event | category | flops | bytes accessed | tf_op | source)
XLA Modules:
  0.0 661.3 jit_solution(10520855624558546295)
XLA Ops:
  9.1 84.0 %all-gather.7.cloned.1.call-done.a_ref = bf16[512,4096]{1,0:T(8,128)(2,1)} async-done(((bf16[128,4096]{1,0:T(8,128)(2,1)}), bf16[512,4096]{1,0:T(8,128)(2,1)}) %all-gather.7.cloned.1.call-update) | async-done | bytes 4194320 | tf_op jit(solution)/shard_map/all_gather | solution.py:184
  93.1 21.8 %shard_map.111 = bf16[3,512,1024]{2,1,0:T(8,128)(2,1)S(1)} custom-call(bf16[512,4096]{1,0:T(8,128)(2,1)} %all-gather.7.cloned.1.call-done.a_ref, bf16[3,4096,1024]{2,1,0:T(8,128)(2,1)} %bitcast.113, bf16[3,32,1,1024]{3,2,1,0:T(2,128)(2,1)S(1)} %broadcast_in_dim.66.m_ref), custom_call_target="tpu_custom_call" | custom-call | flops 12884901888 | bytes 40894464 | tf_op jit(solution)/shard_map/pallas_call | solution.py:66
  120.9 53.1 %all-gather.9.cloned.1.call-done = bf16[512,4096]{1,0:T(8,128)(2,1)} async-done(((bf16[128,4096]{1,0:T(8,128)(2,1)}), bf16[512,4096]{1,0:T(8,128)(2,1)}) %all-gather.9.cloned.1.call-update) | async-done | bytes 4194320 | tf_op jit(solution)/shard_map/all_gather | solution.py:215
  174.0 8.2 %shard_map.113 = f32[512,1024]{1,0:T(8,128)S(1)} custom-call(bf16[1,512,4096]{2,1,0:T(8,128)(2,1)} %bitcast.117, bf16[1,1024,4096]{2,1,0:T(8,128)(2,1)} %bitcast.115, bf16[1,8,1,4096]{3,2,1,0:T(2,128)(2,1)S(1)} %broadcast_in_dim.67.m_ref), custom_call_target="tpu_custom_call" | custom-call | flops 4294967296 | bytes 14680064 | tf_op jit(solution)/shard_map/pallas_call | solution.py:95
  184.0 3.5 select_convert_fusion.1
  189.5 2.9 fusion.7
  192.4 9.9 %all-gather.11.cloned.1.call-done = bf16[64,128,128]{2,1,0:T(8,128)(2,1)} async-done(((bf16[8,128,128]{2,1,0:T(8,128)(2,1)}), bf16[64,128,128]{2,1,0:T(8,128)(2,1)}) %all-gather.11.cloned.1.call-update) | async-done | bytes 2097168 | tf_op jit(solution)/shard_map/all_gather | solution.py:121
  211.7 7.3 %shard_map.112 = bf16[1,512,4096]{2,1,0:T(8,128)(2,1)S(1)} custom-call(bf16[512,1024]{1,0:T(8,128)(2,1)S(1)} %copy.103.a_ref, bf16[1,1024,4096]{2,1,0:T(8,128)(2,1)} %bitcast.116, bf16[1,8,1,4096]{3,2,1,0:T(2,128)(2,1)S(1)} %broadcast_in_dim.67.m_ref), custom_call_target="tpu_custom_call" | custom-call | flops 4294967296 | bytes 16777216 | tf_op jit(solution)/shard_map/pallas_call | solution.py:66
  227.9 3.0 fusion.4
  233.2 4.8 fusion.13
  240.1 5.7 all-gather.13.cloned.1.call-done
  245.8 8.0 %while.23 = (s32[]{:T(128)}, f32[8,128,128]{2,1,0:T(8,128)S(1)}, s32[]{:T(128)}, bf16[8,8,128,128]{3,2,1,0:T(8,128)(2,1)}, s32[]{:T(128)}, /*index=5*/s32[]{:T(128)}, s32[]{:T(128)}, s32[]{:T(128)}) while((s32[]{:T(128)}, f32[8,128,128]{2,1,0:T(8,128)S(1)}, s32[]{:T(128)}, bf16[8,8,128,128]{3,2,1,0:T(8,128)(2,1)}, s32[]{:T(128)}, ...), condition=%wide.region_6.7_spmd, body=%wide.region_5.6_spmd.sunk | while | flops 262150 | bytes 1310855 | solution.py:143
  253.8 3.9 fusion.3
  259.4 3.9 add_convert_fusion.1
  265.9 21.3 %shard_map.114 = bf16[512,4096]{1,0:T(8,128)(2,1)} custom-call(bf16[3,512,1024]{2,1,0:T(8,128)(2,1)S(1)} %pad_maximum_fusion.a_ref, bf16[3,4096,1024]{2,1,0:T(8,128)(2,1)} %bitcast.114, bf16[3,32,1,1024]{3,2,1,0:T(2,128)(2,1)S(1)} %broadcast_in_dim.66.m_ref), custom_call_target="tpu_custom_call" | custom-call | flops 12884901888 | bytes 41943040 | tf_op jit(solution)/shard_map/pallas_call | solution.py:95
  288.4 8.9 %convert_bitcast_fusion.1 = bf16[4096,1024]{0,1:T(8,128)(2,1)} fusion(bf16[512,1024]{0,1:T(8,128)(2,1)S(1)} %bitcast.107, bf16[512,4096]{1,0:T(8,128)(2,1)} %all-gather.9.cloned.1.call-done), kind=kOutput, calls=%fused_computation.3 | convolution fusion | flops 4299161600 | bytes 13631488 | tf_op jit(solution)/shard_map/tm,tf->mf/dot_general | solution.py:221
  298.5 20.7 %convert_bitcast_fusion = bf16[4096,3,1024]{0,2,1:T(8,128)(2,1)} fusion(bf16[512,4096]{1,0:T(8,128)(2,1)} %all-gather.7.cloned.1.call-done.a_ref, bf16[1,512,1024]{2,1,0:T(8,128)(2,1)S(1)} %copy-done.20, bf16[1,512,1024]{2,1,0:T(8,128)(2,1)S(1)} %copy.105, bf16[1,512,1024]{2,1,0:T(8,128)(2,1)S(1)} %copy-done.18), kind=kOutput, calls=%fused_computation.2 | convolution fusion | flops 12900630528 | bytes 32505856 | tf_op jit(solution)/shard_map/tm,ptc->mpc/dot_general | solution.py:262
  320.0 3.6 broadcast_in_dim.64
  323.6 8.0 %reshape.74 = f32[512,3,1024]{0,2,1:T(8,128)} reshape(f32[4,128,3,8,128]{1,0,4,3,2:T(4,128)} %broadcast_in_dim.64) | data formatting | bytes 12582912 | tf_op jit(solution)/shard_map/reshape | solution.py:270
  334.2 70.1 %reduce-scatter.7.cloned.1.call-done = bf16[128,4096]{1,0:T(8,128)(2,1)} async-done(((bf16[512,4096]{1,0:T(8,128)(2,1)}), bf16[128,4096]{1,0:T(8,128)(2,1)}) %reduce-scatter.7.cloned.1.call-update) | async-done | bytes 1048592 | tf_op jit(solution)/shard_map/reduce_scatter | solution.py:272
  406.7 72.8 %reduce-scatter.11.cloned.1.call-done = bf16[512,1024]{0,1:T(8,128)(2,1)} async-done(((bf16[4096,1024]{0,1:T(8,128)(2,1)}), bf16[512,1024]{0,1:T(8,128)(2,1)}) %reduce-scatter.11.cloned.1.call-update) | async-done | bytes 1048592 | tf_op jit(solution)/shard_map/reduce_scatter | solution.py:222
  482.5 158.1 %reduce-scatter.9.cloned.1.call-done = bf16[512,3,1024]{0,2,1:T(8,128)(2,1)} async-done(((bf16[4096,3,1024]{0,2,1:T(8,128)(2,1)}), bf16[512,3,1024]{0,2,1:T(8,128)(2,1)}) %reduce-scatter.9.cloned.1.call-update) | async-done | bytes 3145744 | tf_op jit(solution)/shard_map/reduce_scatter | solution.py:263
  640.5 7.4 %multiply_multiply_fusion = f32[512,3,1024]{0,2,1:T(8,128)} fusion(f32[512,3,1024]{0,2,1:T(8,128)} %reshape.74, bf16[512,3,1024]{0,2,1:T(8,128)(2,1)} %reduce-scatter.9.cloned.1.call-done), kind=kLoop, calls=%fused_computation.6 | loop fusion | flops 4718592 | bytes 15728640 | tf_op jit(solution)/shard_map/mul | solution.py:271
  647.9 6.6 copy.91
  (116 shorter events, 56.9 us)
Async XLA Ops:
  7.2 1.9 copy-start.24
  7.2 1.9 copy-start.25
  7.2 85.9 %all-gather.7.cloned.1.call-start = ((), (), s32[]{:S(2)}) async-start(), calls=%async_computation.4 | async-start | bytes 5242880 | tf_op jit(solution)/shard_map/all_gather | solution.py:184
  7.9 166.1 %all-gather.9.cloned.1.call-start = ((), (), s32[]{:S(2)}) async-start(), calls=%async_computation.6 | async-start | bytes 5242880 | tf_op jit(solution)/shard_map/all_gather | solution.py:215
  8.7 193.7 %all-gather.11.cloned.1.call-start = ((), (), s32[]{:S(2)}) async-start(), calls=%async_computation.10 | async-start | bytes 2359296 | tf_op jit(solution)/shard_map/all_gather | solution.py:121
  116.1 3.2 copy-start.26
  119.2 126.5 %all-gather.13.cloned.1.call-start = ((), (), s32[]{:S(2)}) async-start(), calls=%async_computation.11 | async-start | bytes 2359296 | tf_op jit(solution)/shard_map/all_gather | solution.py:134
  184.0 5.5 copy-start.9
  187.5 2.0 copy-start.5
  203.6 2.9 copy-start.4
  207.8 3.9 copy-start.16
  211.1 120.6 %reduce-scatter.5.cloned.1.call-start = ((), (), s32[]{:S(2)}) async-start(), calls=%async_computation.5 | async-start | bytes 5242880 | tf_op jit(solution)/shard_map/reduce_scatter | solution.py:208
  218.9 2.0 copy-start
  220.9 1.6 copy-start.2
  220.9 183.3 %reduce-scatter.7.cloned.1.call-start = ((), (), s32[]{:S(2)}) async-start(), calls=%async_computation.7 | async-start | bytes 5242880 | tf_op jit(solution)/shard_map/reduce_scatter | solution.py:272
  222.5 2.8 copy-start.12
  225.3 2.6 copy-start.3
  233.2 4.9 copy-start.6
  245.8 8.0 %copy-start.10 = (bf16[64,8,8,128]{3,2,1,0:T(8,128)(2,1)S(1)}, bf16[64,8,8,128]{3,2,1,0:T(8,128)(2,1)}, u32[]{:S(2)}) copy-start(bf16[64,8,8,128]{3,2,1,0:T(8,128)(2,1)} %copy-done.8) | copy-start | bytes 3145732
  263.3 1.6 copy-start.18
  287.2 192.3 %reduce-scatter.11.cloned.1.call-start = ((), (), s32[]{:S(2)}) async-start(), calls=%async_computation.9 | async-start | bytes 9437184 | tf_op jit(solution)/shard_map/reduce_scatter | solution.py:222
  297.3 343.2 %reduce-scatter.9.cloned.1.call-start = ((), (), s32[]{:S(2)}) async-start(), calls=%async_computation.8 | async-start | bytes 28311552 | tf_op jit(solution)/shard_map/reduce_scatter | solution.py:263
  323.6 8.1 %copy-start.14 = (bf16[128,4096]{1,0:T(8,128)(2,1)S(1)}, bf16[128,4096]{1,0:T(8,128)(2,1)}, u32[]{:S(2)}) copy-start(bf16[128,4096]{1,0:T(8,128)(2,1)} %param.12) | copy-start | bytes 3145732
  331.6 72.7 %copy-start.15 = (bf16[128,4096]{1,0:T(8,128)(2,1)S(1)}, bf16[128,4096]{1,0:T(8,128)(2,1)}, u32[]{:S(2)}) copy-start(bf16[128,4096]{1,0:T(8,128)(2,1)} %param.19) | copy-start | bytes 3145732
  (11 other events, 13.1 us)
Sparse Core Ops, SparseCore 0:
  9.6 83.4 all-gather.6
  94.7 79.2 all-gather.8
  175.9 26.4 all-gather.10
  211.2 34.5 all-gather.12
  247.9 76.7 reduce-scatter.4
  327.0 77.2 reduce-scatter.6
  407.7 71.7 reduce-scatter.10
  483.6 156.8 reduce-scatter.8
